TPU v7x, 128 devices: a whole 4x4x4 slice. The times are simulated.
128 devices in a mesh: group: 8 (over z, core), member: 16 (over y, x).
Axes of the slice: x: 4, y: 4, z: 4, core: 2. Of those that a mesh axis runs over, the one named last changes fastest.
Arguments:
- embeddings: bfloat16 [65536, 1024], P(('group', 'member')), may hold values from -70 to 70
- coarse_ids: int32 [65536, 1], P(('group', 'member')), may hold values from 0 to 127; in each aligned block of 512 rows (0 to 511, 512 to 1023, ...) at most 8 rows name the same one
- centroid_seeds: bfloat16 [4096, 1024], P('group'), may hold values from -1 to 1
Outputs:
- refined_centroids: float32 [4096, 1024], P(('group', 'member'))
- row_energy: float32 [65536], P(('group', 'member'))
Inputs may be any that keep to these rules, and one draw needn't show every extreme that they name: `coarse_ids`: in the rows of one device no coarse cluster is named by more than 8 rows.
All inputs are finite; a program needn't handle non-finite values.
Results may differ from a plain program's by a relative error of at most 0.00092.
Values may be sent and summed in bfloat16 or wider, within the bound.
No kernel may reach another device: no remote copies, remote signals or barrier semaphores. Data moves between devices by JAX's collectives and lax.ppermute only.
A program may use at most 64 MiB of HBM per device.

v0:
```python
import math

import jax
import jax.numpy as jnp
from jax import lax
from jax.sharding import PartitionSpec as P

K = 512
ITERS = 2


smoothing_scale = 0.004
prior_mass = 32.0


def shards(embeddings, coarse_ids, centroid_seeds):
    rows_dev, features = embeddings.shape
    groups = lax.axis_size("group")
    members = lax.axis_size("member")
    clusters = groups * members
    capacity = 2 * rows_dev // clusters
    share_rows = K // members
    first_row = lax.axis_index("member") * share_rows
    widened = embeddings.astype(jnp.float32)
    unit_rows = (
        widened
        * lax.rsqrt(jnp.mean(widened * widened, axis=1, keepdims=True) + 1e-06)
        / math.sqrt(features)
    ).astype(jnp.bfloat16)
    cluster_of = coarse_ids[:, 0]
    onehot = (cluster_of[:, None] == jnp.arange(clusters, dtype=jnp.int32)[None, :]).astype(
        jnp.int32
    )
    row_rank = jnp.sum((jnp.cumsum(onehot, axis=0) - onehot) * onehot, axis=1)
    slot_of = cluster_of * capacity + row_rank
    source = (
        jnp.full((clusters * capacity,), -1, jnp.int32)
        .at[slot_of]
        .set(jnp.arange(rows_dev, dtype=jnp.int32))
    )
    filled = source >= 0
    packed = jnp.where(
        filled[:, None], unit_rows[jnp.maximum(source, 0)], jnp.zeros((), jnp.bfloat16)
    )
    row_flags = filled.astype(jnp.bfloat16)
    arrived, arrived_flags = (
        lax.all_to_all(packed, ("group", "member"), split_axis=0, concat_axis=0, tiled=True),
        lax.all_to_all(row_flags, ("group", "member"), split_axis=0, concat_axis=0, tiled=True),
    )
    slot_mask = arrived_flags.astype(jnp.float32)
    centroids = centroid_seeds.astype(jnp.float32)
    updated = lax.dynamic_slice_in_dim(centroids, first_row, share_rows, 0)
    closing_log_partition = jnp.zeros((clusters * capacity,), jnp.float32)
    for iteration in range(ITERS):
        prototype_lowbits = centroids.astype(jnp.bfloat16)
        half_quadratic_length = 0.5 * jnp.sum(centroids * centroids, axis=1)
        similarity_logits = (
            jnp.dot(arrived, prototype_lowbits.T, preferred_element_type=jnp.float32)
            - half_quadratic_length[None, :]
        ) / smoothing_scale
        row_max = jnp.max(similarity_logits, axis=1, keepdims=True)
        powers = jnp.exp(similarity_logits - row_max)
        row_sum = jnp.sum(powers, axis=1, keepdims=True)
        weights = (powers / row_sum * slot_mask[:, None]).astype(jnp.bfloat16)
        closing_log_partition = row_max[:, 0] + jnp.log(row_sum[:, 0])
        weighted = jnp.einsum("rk,rd->kd", weights, arrived, preferred_element_type=jnp.float32)
        masses = jnp.sum(weights.astype(jnp.float32), axis=0)
        weighted_all, masses_all = lax.psum((weighted, masses), "member")
        centroids = (weighted_all + prior_mass * centroids) / (masses_all + prior_mass)[:, None]
        updated = lax.dynamic_slice_in_dim(centroids, first_row, share_rows, 0)
    prototype_position_cost = smoothing_scale * closing_log_partition
    returned = lax.all_to_all(
        prototype_position_cost, ("group", "member"), split_axis=0, concat_axis=0, tiled=True
    )
    row_energy = returned[slot_of]
    return (updated, row_energy)


def solution(mesh):
    in_specs = (P(("group", "member"), None), P(("group", "member"), None), P("group", None))
    out_specs = (P(("group", "member"), None), P(("group", "member")))
    return jax.shard_map(shards, mesh=mesh, in_specs=in_specs, out_specs=out_specs, check_vma=False)
```

profile of v0, /device:TPU:1, one launch (start us, length us, event | category | flops | bytes accessed | tf_op | source)
XLA Modules:
  0.0 269.3 jit_solution(15785555380074873003)
XLA Ops:
  7.2 0.0 copy-start
  7.2 0.9 copy.8
  8.1 0.2 fusion.21
  8.4 0.9 fusion.20
  9.3 0.7 compare_select_fusion
  10.0 2.4 scatter_custom_fusion
  12.4 0.7 reshape.117
  13.2 11.5 %all-to-all-start.1 = ((bf16[128,8,1]{1,2,0:T(2,128)(2,1)}), bf16[128,8,1]{1,2,0:T(2,128)(2,1)S(1)}, u32[]{:S(2)}, u32[]{:S(2)}) async-start(bf16[128,8,1]{1,2,0:T(2,128)(2,1)} %reshape.117), calls=%async_computation.1 | async-start | bytes 131072 | tf_op jit(solution)/shard_map/all_to_all | solution.py:48
  24.7 0.1 broadcast_in_dim.19
  24.8 0.0 copy-done
  24.8 0.3 fusion
  25.1 0.3 fusion.2
  25.4 4.1 %gather_fusion = bf16[1024,1024]{1,0:T(8,128)(2,1)S(1)} fusion(bf16[512,1024]{1,0:T(8,128)(2,1)S(1)} %fusion.2, s32[1024]{0:T(1024)S(1)} %maximum_clamp_fusion), kind=kCustom, calls=%fused_computation | custom fusion | bytes 4198400 | tf_op jit(solution)/shard_map/gather | solution.py:43
  29.5 1.6 bitcast_select_fusion
  31.1 3.1 %all-to-all-done.1 = bf16[128,8,1]{1,2,0:T(2,128)(2,1)S(1)} async-done(((bf16[128,8,1]{1,2,0:T(2,128)(2,1)}), bf16[128,8,1]{1,2,0:T(2,128)(2,1)S(1)}, u32[]{:S(2)}, u32[]{:S(2)}) %all-to-all-start.1) | async-done | bytes 2080 | tf_op jit(solution)/shard_map/all_to_all | solution.py:48
  34.2 6.6 %all-to-all-start = ((bf16[128,8,1024]{2,1,0:T(8,128)(2,1)}), bf16[128,8,1024]{2,1,0:T(8,128)(2,1)S(1)}, u32[]{:S(2)}, u32[]{:S(2)}) async-start(bf16[128,8,1024]{2,1,0:T(8,128)(2,1)} %bitcast_select_fusion), calls=%async_computation | async-start | bytes 4194304 | tf_op jit(solution)/shard_map/all_to_all | solution.py:47
  40.8 0.0 all-reduce.3.cloned.1.call-start
  40.9 0.3 fusion.3
  41.2 0.2 convert_reduce_fusion.2
  41.4 0.1 reshape.91
  41.5 29.1 %all-to-all-done = bf16[128,8,1024]{2,1,0:T(8,128)(2,1)S(1)} async-done(((bf16[128,8,1024]{2,1,0:T(8,128)(2,1)}), bf16[128,8,1024]{2,1,0:T(8,128)(2,1)S(1)}, u32[]{:S(2)}, u32[]{:S(2)}) %all-to-all-start) | async-done | bytes 2097184 | tf_op jit(solution)/shard_map/all_to_all | solution.py:47
  70.5 1.3 fusion.14
  71.8 0.5 fusion.16
  72.3 0.8 convert_reduce_fusion.1
  73.1 0.0 copy-done.2
  73.1 2.6 fusion.10
  75.7 0.0 all-reduce.3.cloned.1.call-update
  75.8 0.0 all-reduce.5.cloned.1.call-start
  75.8 31.1 %psum.29 = f32[512]{0:T(512)S(1)} all-reduce(f32[512]{0:T(512)S(1)} %get-tuple-element.6), channel_id=1, replica_groups=mesh['group'=8,'member'=16] {'member'}, use_global_device_ids=true, to_apply=%region_10.11 | all-reduce | flops 512 | bytes 4096 | tf_op jit(solution)/shard_map/psum | solution.py:68
  106.9 55.1 %all-reduce.3.cloned.1.call-done = f32[512,1024]{1,0:T(8,128)} async-done(((f32[512,1024]{1,0:T(8,128)}), f32[512,1024]{1,0:T(8,128)}) %all-reduce.3.cloned.1.call-update) | async-done | bytes 2097168 | tf_op jit(solution)/shard_map/psum | solution.py:68
  162.0 2.2 multiply_reduce_fusion
  164.3 0.0 copy-done.3
  164.3 1.3 fusion.15
  165.6 0.5 fusion.17
  166.1 0.8 convert_reduce_fusion
  166.9 2.6 fusion.6
  169.5 0.0 all-reduce.5.cloned.1.call-update
  169.5 0.7 mul.98
  170.2 9.2 %all-to-all-start.2 = ((f32[128,8,1]{1,2,0:T(1,128)}), f32[128,8,1]{1,2,0:T(1,128)S(1)}, u32[]{:S(2)}, u32[]{:S(2)}) async-start(f32[128,8,1]{1,2,0:T(1,128)} %bitcast.9), calls=%async_computation.2 | async-start | bytes 131072 | tf_op jit(solution)/shard_map/all_to_all | solution.py:72
  179.4 33.9 %psum.31 = f32[512]{0:T(512)S(1)} all-reduce(f32[512]{0:T(512)S(1)} %get-tuple-element.2), channel_id=1, replica_groups=mesh['group'=8,'member'=16] {'member'}, use_global_device_ids=true, to_apply=%region_16.17 | all-reduce | flops 512 | bytes 4096 | tf_op jit(solution)/shard_map/psum | solution.py:68
  213.4 0.1 dynamic-slice
  213.4 0.0 all-to-all-done.2
  213.4 0.5 broadcast.125
  214.0 0.8 reduce.7
  214.8 0.1 all_to_all.26
  214.9 3.4 %gather_fusion.1 = f32[512]{0:T(512)} fusion(f32[1024]{0:T(1024)S(1)} %all_to_all.26, s32[1024]{0:T(1024)S(1)} %pad_clamp_fusion), kind=kCustom, calls=%fused_computation.1 | custom fusion | bytes 6144 | tf_op jit(solution)/shard_map/gather | solution.py:75
  218.3 42.5 %all-reduce.5.cloned.1.call-done = f32[512,1024]{1,0:T(8,128)} async-done(((f32[512,1024]{1,0:T(8,128)}), f32[512,1024]{1,0:T(8,128)}) %all-reduce.5.cloned.1.call-update) | async-done | bytes 2097168 | tf_op jit(solution)/shard_map/psum | solution.py:68
  260.8 1.6 fusion.23
  (20 shorter events, 0.2 us)
Async XLA Ops:
  7.2 17.6 %copy-start = (bf16[512,1024]{1,0:T(8,128)(2,1)S(1)}, bf16[512,1024]{1,0:T(8,128)(2,1)}, u32[]{:S(2)}) copy-start(bf16[512,1024]{1,0:T(8,128)(2,1)} %param.3) | copy-start | bytes 3145732
  13.2 21.0 %all-to-all-start.1 = ((bf16[128,8,1]{1,2,0:T(2,128)(2,1)}), bf16[128,8,1]{1,2,0:T(2,128)(2,1)S(1)}, u32[]{:S(2)}, u32[]{:S(2)}) async-start(bf16[128,8,1]{1,2,0:T(2,128)(2,1)} %reshape.117), calls=%async_computation.1 | async-start | bytes 131072 | tf_op jit(solution)/shard_map/all_to_all | solution.py:48
  31.1 9.8 %copy-start.1 = (bf16[512,1024]{1,0:T(8,128)(2,1)S(1)}, bf16[512,1024]{1,0:T(8,128)(2,1)}, u32[]{:S(2)}) copy-start(bf16[512,1024]{1,0:T(8,128)(2,1)} %param.5) | copy-start | bytes 3145732
  34.2 36.3 %all-to-all-start = ((bf16[128,8,1024]{2,1,0:T(8,128)(2,1)}), bf16[128,8,1024]{2,1,0:T(8,128)(2,1)S(1)}, u32[]{:S(2)}, u32[]{:S(2)}) async-start(bf16[128,8,1024]{2,1,0:T(8,128)(2,1)} %bitcast_select_fusion), calls=%async_computation | async-start | bytes 4194304 | tf_op jit(solution)/shard_map/all_to_all | solution.py:47
  40.8 121.2 %all-reduce.3.cloned.1.call-start = ((), (), s32[]{:S(2)}) async-start(), calls=%async_computation.3 | async-start | bytes 4194304 | tf_op jit(solution)/shard_map/psum | solution.py:68
  70.5 2.6 copy-start.2
  75.8 185.0 %all-reduce.5.cloned.1.call-start = ((), (), s32[]{:S(2)}) async-start(), calls=%async_computation.4 | async-start | bytes 4194304 | tf_op jit(solution)/shard_map/psum | solution.py:68
  162.0 2.3 copy-start.3
  170.2 43.2 %all-to-all-start.2 = ((f32[128,8,1]{1,2,0:T(1,128)}), f32[128,8,1]{1,2,0:T(1,128)S(1)}, u32[]{:S(2)}, u32[]{:S(2)}) async-start(f32[128,8,1]{1,2,0:T(1,128)} %bitcast.9), calls=%async_computation.2 | async-start | bytes 131072 | tf_op jit(solution)/shard_map/all_to_all | solution.py:72
Sparse Core Ops, SparseCore 0:
  75.9 86.0 all-reduce.2
  169.6 91.1 all-reduce.4
where the time goes:
time: 270 us; the launch traced here: 269 us
  waiting for transfers between devices  130 us (48%)
  blocking collectives  65.1 us (24%)
  starting transfers between devices  27.3 us (10%)
  between operations  14.3 us (5%)
  local copies, waits for them, and re-layouts  13.2 us (5%)
  other arithmetic  11.8 us (4%)
  matrix products  7.79 us (3%)
    psum x2, waiting for transfers between devices, shards(): weighted_all, masses_all = lax.psum((weighted, masses), 'member')  97.6 us
    psum x2, blocking collectives, shards(): weighted_all, masses_all = lax.psum((weighted, masses), 'member')  65.1 us
    all_to_all x1, waiting for transfers between devices, shards(): lax.all_to_all(packed, ('group', 'member'), split_axis=0, concat_axis=0,...  29.1 us
    all_to_all x1, starting transfers between devices, shards(): lax.all_to_all(row_flags, ('group', 'member'), split_axis=0, concat_axis=...  11.5 us
    all_to_all x1, starting transfers between devices, shards(): lax.all_to_all(prototype_position_cost, ('group', 'member'), split_axis=0...  9.17 us
    all_to_all x1, starting transfers between devices, shards(): lax.all_to_all(packed, ('group', 'member'), split_axis=0, concat_axis=0,...  6.62 us
  transfers between devices with their start and end apart: 5, of which 4 were waited for; matrix products, arithmetic and copies ran while one was open for 5% of the time, Pallas kernels for 0%

commit v1 on v0

--- a/solution.py
+++ b/solution.py
@@ -11,6 +11,7 @@
 
 smoothing_scale = 0.004
 prior_mass = 32.0
+empty_mark = 2.0
 
 
 def shards(embeddings, coarse_ids, centroid_seeds):
@@ -39,21 +40,18 @@
         .set(jnp.arange(rows_dev, dtype=jnp.int32))
     )
     filled = source >= 0
-    packed = jnp.where(
-        filled[:, None], unit_rows[jnp.maximum(source, 0)], jnp.zeros((), jnp.bfloat16)
-    )
-    row_flags = filled.astype(jnp.bfloat16)
-    arrived, arrived_flags = (
-        lax.all_to_all(packed, ("group", "member"), split_axis=0, concat_axis=0, tiled=True),
-        lax.all_to_all(row_flags, ("group", "member"), split_axis=0, concat_axis=0, tiled=True),
-    )
-    slot_mask = arrived_flags.astype(jnp.float32)
-    centroids = centroid_seeds.astype(jnp.float32)
-    updated = lax.dynamic_slice_in_dim(centroids, first_row, share_rows, 0)
+    empty_row = jnp.where(
+        jnp.arange(features) == 0, jnp.bfloat16(empty_mark), jnp.bfloat16(0)
+    ).astype(jnp.bfloat16)
+    packed = jnp.where(filled[:, None], unit_rows[jnp.maximum(source, 0)], empty_row[None, :])
+    arrived = lax.all_to_all(packed, ("group", "member"), split_axis=0, concat_axis=0, tiled=True)
+    slot_mask = (arrived[:, 0].astype(jnp.float32) < 1.5).astype(jnp.float32)
+    seeds = centroid_seeds.astype(jnp.float32)
+    own = lax.dynamic_slice_in_dim(seeds, first_row, share_rows, 0)
+    prototype_lowbits = centroid_seeds
+    half_quadratic_length = 0.5 * jnp.sum(seeds * seeds, axis=1)
     closing_log_partition = jnp.zeros((clusters * capacity,), jnp.float32)
     for iteration in range(ITERS):
-        prototype_lowbits = centroids.astype(jnp.bfloat16)
-        half_quadratic_length = 0.5 * jnp.sum(centroids * centroids, axis=1)
         similarity_logits = (
             jnp.dot(arrived, prototype_lowbits.T, preferred_element_type=jnp.float32)
             - half_quadratic_length[None, :]
@@ -65,15 +63,34 @@
         closing_log_partition = row_max[:, 0] + jnp.log(row_sum[:, 0])
         weighted = jnp.einsum("rk,rd->kd", weights, arrived, preferred_element_type=jnp.float32)
         masses = jnp.sum(weights.astype(jnp.float32), axis=0)
-        weighted_all, masses_all = lax.psum((weighted, masses), "member")
-        centroids = (weighted_all + prior_mass * centroids) / (masses_all + prior_mass)[:, None]
-        updated = lax.dynamic_slice_in_dim(centroids, first_row, share_rows, 0)
+        combined = jnp.concatenate(
+            [
+                weighted.reshape(members, share_rows * features),
+                jnp.pad(masses.reshape(members, share_rows), ((0, 0), (0, 128 - share_rows))),
+            ],
+            axis=1,
+        )
+        reduced = jnp.sum(
+            lax.all_to_all(combined, "member", split_axis=0, concat_axis=0, tiled=True),
+            axis=0,
+            keepdims=True,
+        )
+        weighted_own = reduced[0, : share_rows * features].reshape(share_rows, features)
+        masses_own = reduced[0, share_rows * features : share_rows * features + share_rows]
+        own = (weighted_own + prior_mass * own) / (masses_own + prior_mass)[:, None]
+        if iteration + 1 < ITERS:
+            prototype_lowbits = lax.all_gather(
+                own.astype(jnp.bfloat16), "member", axis=0, tiled=True
+            )
+            half_quadratic_length = lax.all_gather(
+                0.5 * jnp.sum(own * own, axis=1), "member", axis=0, tiled=True
+            )
     prototype_position_cost = smoothing_scale * closing_log_partition
     returned = lax.all_to_all(
         prototype_position_cost, ("group", "member"), split_axis=0, concat_axis=0, tiled=True
     )
     row_energy = returned[slot_of]
-    return (updated, row_energy)
+    return (own, row_energy)
 
 
 def solution(mesh):

time: 270 us -> 217 us (0.80)
  blocking collectives: 65.1 us -> 29.5 us
  waiting for transfers between devices: 130 us -> 95.1 us
  local copies, waits for them, and re-layouts: 13.2 us -> 23 us
  other arithmetic: 11.8 us -> 15 us
    psum x2 -> x0, waiting for transfers between devices: 97.6 us -> none  [shards(): weighted_all, masses_all = lax.psum((weighted, masses), 'member')]
    psum x2 -> x0, blocking collectives: 65.1 us -> none  [shards(): weighted_all, masses_all = lax.psum((weighted, masses), 'member')]
    all_to_all x1 -> x2, waiting for transfers between devices: 3.15 us -> 55.4 us  [shards(): lax.all_to_all(combined, 'member', split_axis=0, concat_axis=0, tiled=True)]
    unnamed x0 -> x1, blocking collectives: none -> 29.5 us
    all_gather x0 -> x1, waiting for transfers between devices: none -> 8.16 us  [shards(): lax.all_gather(own.astype(jnp.bfloat16), 'member', axis=0, tiled=True)]
    all_to_all x1, starting transfers between devices: 6.62 us -> 11.5 us  [shards(): lax.all_to_all(packed, ('group', 'member'), split_axis=0, concat_axis=0,...]
    all_to_all x1 -> x2, local copies, waits for them, and re-layouts: 0.75 us -> 5.59 us  [shards(): lax.all_to_all(combined, 'member', split_axis=0, concat_axis=0, tiled=True)]
    reshape x0 -> x4, local copies, waits for them, and re-layouts: none -> 3.64 us  [the longest x2 3.49 us: shards(): weighted.reshape(members, share_rows * features)]
  transfers between devices with their start and end apart: 5 -> 5, of which waited for: 4 -> 5; matrix products, arithmetic and copies ran while one was open for 5% -> 5% of each run, Pallas kernels for 0% -> 0%
where the time goes in v1:
time: 217 us; the launch traced here: 216 us
  waiting for transfers between devices  95.1 us (44%)
  blocking collectives  29.5 us (14%)
  starting transfers between devices  29 us (13%)
  local copies, waits for them, and re-layouts  23 us (11%)
  other arithmetic  15 us (7%)
  between operations  15 us (7%)
  matrix products  9.69 us (4%)
    all_to_all x2, waiting for transfers between devices, shards(): lax.all_to_all(combined, 'member', split_axis=0, concat_axis=0, tiled=True)  55.4 us
    unnamed x1, blocking collectives  29.5 us
    all_to_all x1, waiting for transfers between devices, shards(): lax.all_to_all(packed, ('group', 'member'), split_axis=0, concat_axis=0,...  29.4 us
    all_to_all x1, starting transfers between devices, shards(): lax.all_to_all(packed, ('group', 'member'), split_axis=0, concat_axis=0,...  11.5 us
    all_to_all x1, starting transfers between devices, shards(): lax.all_to_all(prototype_position_cost, ('group', 'member'), split_axis=0...  9.25 us
    all_to_all x2, starting transfers between devices, shards(): lax.all_to_all(combined, 'member', split_axis=0, concat_axis=0, tiled=True)  8.25 us
    all_gather x1, waiting for transfers between devices, shards(): lax.all_gather(own.astype(jnp.bfloat16), 'member', axis=0, tiled=True)  8.16 us
    all_to_all x2, local copies, waits for them, and re-layouts, shards(): lax.all_to_all(combined, 'member', split_axis=0, concat_axis=0, tiled=True)  5.59 us
  transfers between devices with their start and end apart: 5, of which 5 were waited for; matrix products, arithmetic and copies ran while one was open for 5% of the time, Pallas kernels for 0%

profile of v1, /device:TPU:1, one launch (start us, length us, event | category | flops | bytes accessed | tf_op | source)
XLA Modules:
  0.0 216.3 jit_solution(2179344163561366257)
XLA Ops:
  7.2 0.9 copy.11
  8.1 0.2 fusion.9
  8.4 0.9 fusion.8
  9.3 0.7 compare_select_fusion
  10.0 2.4 %scatter_custom_fusion = s32[1024]{0:T(1024)S(1)} fusion(s32[512]{0:T(512)S(1)} %bitcast.50, s32[512]{0:T(512)S(1)} %iota.16, s32[]{:T(128)} %constant.19.clone.1), kind=kCustom, calls=%fused_computation.50 | custom fusion | bytes 4100 | tf_op jit(solution)/shard_map/scatter | solution.py:40
  12.5 0.3 fusion
  12.8 0.3 fusion.2
  13.2 4.1 %gather_fusion = bf16[1024,1024]{1,0:T(8,128)(2,1)S(1)} fusion(bf16[512,1024]{1,0:T(8,128)(2,1)S(1)} %fusion.2, s32[1024]{0:T(1024)S(1)} %maximum_clamp_fusion), kind=kCustom, calls=%fused_computation | custom fusion | bytes 4198400 | tf_op jit(solution)/shard_map/gather | solution.py:46
  17.3 1.6 bitcast_select_fusion
  18.8 11.5 %all-to-all-start = ((bf16[128,8,1024]{2,1,0:T(8,128)(2,1)}), bf16[128,8,1024]{2,1,0:T(8,128)(2,1)S(1)}, u32[]{:S(2)}, u32[]{:S(2)}) async-start(bf16[128,8,1024]{2,1,0:T(8,128)(2,1)} %bitcast_select_fusion), calls=%async_computation | async-start | bytes 4194304 | tf_op jit(solution)/shard_map/all_to_all | solution.py:47
  30.3 0.3 multiply_reduce_fusion
  30.6 29.4 %all-to-all-done = bf16[128,8,1024]{2,1,0:T(8,128)(2,1)S(1)} async-done(((bf16[128,8,1024]{2,1,0:T(8,128)(2,1)}), bf16[128,8,1024]{2,1,0:T(8,128)(2,1)S(1)}, u32[]{:S(2)}, u32[]{:S(2)}) %all-to-all-start) | async-done | bytes 2097184 | tf_op jit(solution)/shard_map/all_to_all | solution.py:47
  60.0 0.2 convert_reduce_fusion.2
  60.2 1.3 fusion.3
  61.5 0.5 fusion.5
  62.0 0.8 convert_reduce_fusion.1
  62.8 2.6 %fusion.21 = f32[512,1024]{1,0:T(8,128)} fusion(bf16[1024,512]{0,1:T(8,128)(2,1)S(1)} %get-tuple-element.7, bf16[128,8,1024]{2,1,0:T(8,128)(2,1)S(1)} %all-to-all-done), kind=kOutput, calls=%fused_computation.62 | convolution fusion | flops 1073741824 | bytes 5242880 | tf_op jit(solution)/shard_map/rk,rd->kd/dot_general | solution.py:64
  65.4 1.7 reshape.116
  67.2 0.1 select_maximum_fusion.1
  67.4 2.8 %all_to_all.26 = f32[16,1,32896]{2,1,0:T(1,128)} reshape(f32[16,32896]{1,0:T(8,128)S(1)} %select_maximum_fusion.1) | data formatting | bytes 4210688 | tf_op jit(solution)/shard_map/all_to_all | solution.py:74
  70.2 3.7 %all-to-all-start.1 = ((f32[16,1,32896]{2,1,0:T(1,128)}), f32[16,1,32896]{2,1,0:T(1,128)S(1)}, u32[]{:S(2)}, u32[]{:S(2)}) async-start(f32[16,1,32896]{2,1,0:T(1,128)} %all_to_all.26), calls=%async_computation.1 | async-start | bytes 4210688 | tf_op jit(solution)/shard_map/all_to_all | solution.py:74
  73.9 1.6 convert_element_type.44
  75.5 28.0 %all-to-all-done.1 = f32[16,1,32896]{2,1,0:T(1,128)S(1)} async-done(((f32[16,1,32896]{2,1,0:T(1,128)}), f32[16,1,32896]{2,1,0:T(1,128)S(1)}, u32[]{:S(2)}, u32[]{:S(2)}) %all-to-all-start.1) | async-done | bytes 2105376 | tf_op jit(solution)/shard_map/all_to_all | solution.py:74
  103.6 1.3 reduce_sum.98
  105.0 0.3 slice_reduce_fusion.1
  105.4 1.1 multiply_reduce_fusion.1
  106.5 0.6 convert_element_type.48
  107.2 0.6 dynamic-slice
  108.5 29.5 %all-reduce.2 = f32[512]{0:T(512)S(1)} all-reduce(f32[512]{0:T(512)S(1)} %multiply_dynamic-update-slice_fusion), channel_id=1, replica_groups=mesh['group'=8,'member'=16] {'member'}, use_global_device_ids=true, to_apply=%add.2 | all-reduce | flops 512 | bytes 4096
  138.0 8.2 %all-gather.2.cloned.1.call-done = bf16[512,1024]{1,0:T(8,128)(2,1)} async-done(((bf16[32,1024]{1,0:T(8,128)(2,1)}), bf16[512,1024]{1,0:T(8,128)(2,1)}) %all-gather.2.cloned.1.call-update) | async-done | bytes 1048592 | tf_op jit(solution)/shard_map/all_gather | solution.py:82
  146.2 3.2 %fusion.4 = (f32[1024]{0:T(1024)S(1)}, f32[1024,512]{0,1:T(8,128)S(1)}) fusion(f32[512]{0:T(512)S(1)} %all-reduce.2, bf16[512,1024]{1,0:T(8,128)(2,1)} %all-gather.2.cloned.1.call-done, bf16[128,8,1024]{2,1,0:T(8,128)(2,1)} %copy-done.2), kind=kOutput, calls=%fused_computation.22 | convolution fusion | flops 1075313664 | bytes 5249024 | tf_op jit(solution)/shard_map/dot_general | solution.py:56
  149.3 0.5 fusion.6
  149.8 0.8 convert_reduce_fusion
  150.7 0.7 mul.109
  151.4 9.2 %all-to-all-start.3 = ((f32[128,8,1]{1,2,0:T(1,128)}), f32[128,8,1]{1,2,0:T(1,128)S(1)}, u32[]{:S(2)}, u32[]{:S(2)}) async-start(f32[128,8,1]{1,2,0:T(1,128)} %bitcast.12), calls=%async_computation.3 | async-start | bytes 131072 | tf_op jit(solution)/shard_map/all_to_all | solution.py:89
  160.6 2.6 %fusion.17 = f32[512,1024]{1,0:T(8,128)} fusion(bf16[1024,512]{0,1:T(8,128)(2,1)S(1)} %get-tuple-element.3, bf16[128,8,1024]{2,1,0:T(8,128)(2,1)S(1)} %copy-done.3), kind=kOutput, calls=%fused_computation.58 | convolution fusion | flops 1073741824 | bytes 5242880 | tf_op jit(solution)/shard_map/rk,rd->kd/dot_general | solution.py:64
  163.3 1.7 reshape.118
  165.1 0.1 select_maximum_fusion
  165.2 2.8 %all_to_all.28 = f32[16,1,32896]{2,1,0:T(1,128)} reshape(f32[16,32896]{1,0:T(8,128)S(1)} %select_maximum_fusion) | data formatting | bytes 4210688 | tf_op jit(solution)/shard_map/all_to_all | solution.py:74
  168.0 2.1 all-to-all-done.3
  170.2 4.5 %all-to-all-start.2 = ((f32[16,1,32896]{2,1,0:T(1,128)}), f32[16,1,32896]{2,1,0:T(1,128)S(1)}, u32[]{:S(2)}, u32[]{:S(2)}) async-start(f32[16,1,32896]{2,1,0:T(1,128)} %all_to_all.28), calls=%async_computation.2 | async-start | bytes 4210688 | tf_op jit(solution)/shard_map/all_to_all | solution.py:74
  174.7 0.5 broadcast.154
  175.2 0.8 reduce.15
  176.1 3.4 %gather_fusion.1 = f32[512]{0:T(512)} fusion(f32[1024]{0:T(1024)S(1)} %all_to_all.31, s32[1024]{0:T(1024)S(1)} %pad_clamp_fusion), kind=kCustom, calls=%fused_computation.1 | custom fusion | bytes 6144 | tf_op jit(solution)/shard_map/gather | solution.py:92
  179.6 27.3 %all-to-all-done.2 = f32[16,1,32896]{2,1,0:T(1,128)S(1)} async-done(((f32[16,1,32896]{2,1,0:T(1,128)}), f32[16,1,32896]{2,1,0:T(1,128)S(1)}, u32[]{:S(2)}, u32[]{:S(2)}) %all-to-all-start.2) | async-done | bytes 2105376 | tf_op jit(solution)/shard_map/all_to_all | solution.py:74
  206.9 1.3 reduce_sum.102
  208.3 0.3 slice_reduce_fusion
  208.7 0.7 add_divide_fusion
  (38 shorter events, 0.9 us)
Async XLA Ops:
  7.2 5.3 %copy-start.1 = (bf16[512,1024]{1,0:T(8,128)(2,1)S(1)}, bf16[512,1024]{1,0:T(8,128)(2,1)}, u32[]{:S(2)}) copy-start(bf16[512,1024]{1,0:T(8,128)(2,1)} %param.3) | copy-start | bytes 3145732
  18.8 11.5 %copy-start = (bf16[512,1024]{1,0:T(8,128)(2,1)S(1)}, bf16[512,1024]{1,0:T(8,128)(2,1)}, u32[]{:S(2)}) copy-start(bf16[512,1024]{1,0:T(8,128)(2,1)} %param.5) | copy-start | bytes 3145732
  18.8 41.2 %all-to-all-start = ((bf16[128,8,1024]{2,1,0:T(8,128)(2,1)}), bf16[128,8,1024]{2,1,0:T(8,128)(2,1)S(1)}, u32[]{:S(2)}, u32[]{:S(2)}) async-start(bf16[128,8,1024]{2,1,0:T(8,128)(2,1)} %bitcast_select_fusion), calls=%async_computation | async-start | bytes 4194304 | tf_op jit(solution)/shard_map/all_to_all | solution.py:47
  60.0 2.8 %copy-start.2 = (bf16[128,8,1024]{2,1,0:T(8,128)(2,1)}, bf16[128,8,1024]{2,1,0:T(8,128)(2,1)S(1)}, u32[]{:S(2)}) copy-start(bf16[128,8,1024]{2,1,0:T(8,128)(2,1)S(1)} %all-to-all-done) | copy-start | bytes 6291460
  70.2 33.4 %all-to-all-start.1 = ((f32[16,1,32896]{2,1,0:T(1,128)}), f32[16,1,32896]{2,1,0:T(1,128)S(1)}, u32[]{:S(2)}, u32[]{:S(2)}) async-start(f32[16,1,32896]{2,1,0:T(1,128)} %all_to_all.26), calls=%async_computation.1 | async-start | bytes 4210688 | tf_op jit(solution)/shard_map/all_to_all | solution.py:74
  73.9 72.3 %all-gather.2.cloned.1.call-start = ((), (), s32[]{:S(2)}) async-start(), calls=%async_computation.4 | async-start | bytes 1114112 | tf_op jit(solution)/shard_map/all_gather | solution.py:82
  75.5 31.6 %copy-start.4 = (u32[128]{0:T(128)S(1)}, u32[128]{0:T(128)}, u32[]{:S(2)}) copy-start(u32[128]{0:T(128)} %constant.61) | copy-start | bytes 1540
  149.8 10.8 %copy-start.3 = (bf16[128,8,1024]{2,1,0:T(8,128)(2,1)S(1)}, bf16[128,8,1024]{2,1,0:T(8,128)(2,1)}, u32[]{:S(2)}) copy-start(bf16[128,8,1024]{2,1,0:T(8,128)(2,1)} %copy-done.2) | copy-start | bytes 6291460
  151.4 18.8 %all-to-all-start.3 = ((f32[128,8,1]{1,2,0:T(1,128)}), f32[128,8,1]{1,2,0:T(1,128)S(1)}, u32[]{:S(2)}, u32[]{:S(2)}) async-start(f32[128,8,1]{1,2,0:T(1,128)} %bitcast.12), calls=%async_computation.3 | async-start | bytes 131072 | tf_op jit(solution)/shard_map/all_to_all | solution.py:89
  170.2 36.7 %all-to-all-start.2 = ((f32[16,1,32896]{2,1,0:T(1,128)}), f32[16,1,32896]{2,1,0:T(1,128)S(1)}, u32[]{:S(2)}, u32[]{:S(2)}) async-start(f32[16,1,32896]{2,1,0:T(1,128)} %all_to_all.28), calls=%async_computation.2 | async-start | bytes 4210688 | tf_op jit(solution)/shard_map/all_to_all | solution.py:74
Sparse Core Ops, SparseCore 0:
  107.3 38.8 all-gather.1

commit v2 on v1

--- a/solution.py
+++ b/solution.py
@@ -34,16 +34,17 @@
     )
     row_rank = jnp.sum((jnp.cumsum(onehot, axis=0) - onehot) * onehot, axis=1)
     slot_of = cluster_of * capacity + row_rank
-    source = (
-        jnp.full((clusters * capacity,), -1, jnp.int32)
-        .at[slot_of]
-        .set(jnp.arange(rows_dev, dtype=jnp.int32))
-    )
-    filled = source >= 0
+    placement = (
+        slot_of[None, :] == jnp.arange(clusters * capacity, dtype=jnp.int32)[:, None]
+    ).astype(jnp.bfloat16)
+    filled = jnp.sum(placement.astype(jnp.float32), axis=1) > 0.5
     empty_row = jnp.where(
         jnp.arange(features) == 0, jnp.bfloat16(empty_mark), jnp.bfloat16(0)
     ).astype(jnp.bfloat16)
-    packed = jnp.where(filled[:, None], unit_rows[jnp.maximum(source, 0)], empty_row[None, :])
+    gathered = jnp.dot(placement, unit_rows, preferred_element_type=jnp.float32).astype(
+        jnp.bfloat16
+    )
+    packed = jnp.where(filled[:, None], gathered, empty_row[None, :])
     arrived = lax.all_to_all(packed, ("group", "member"), split_axis=0, concat_axis=0, tiled=True)
     slot_mask = (arrived[:, 0].astype(jnp.float32) < 1.5).astype(jnp.float32)
     seeds = centroid_seeds.astype(jnp.float32)
@@ -79,12 +80,29 @@
         masses_own = reduced[0, share_rows * features : share_rows * features + share_rows]
         own = (weighted_own + prior_mass * own) / (masses_own + prior_mass)[:, None]
         if iteration + 1 < ITERS:
-            prototype_lowbits = lax.all_gather(
-                own.astype(jnp.bfloat16), "member", axis=0, tiled=True
+            half_own = 0.5 * jnp.sum(own * own, axis=1)
+            high = lax.reduce_precision(half_own, exponent_bits=8, mantissa_bits=7)
+            rest = half_own - high
+            middle = lax.reduce_precision(rest, exponent_bits=8, mantissa_bits=7)
+            low = rest - middle
+            block = jnp.concatenate(
+                [
+                    own.astype(jnp.bfloat16),
+                    jnp.stack([high, middle, low], axis=1).astype(jnp.bfloat16),
+                    jnp.zeros((share_rows, 125), jnp.bfloat16),
+                ],
+                axis=1,
             )
-            half_quadratic_length = lax.all_gather(
-                0.5 * jnp.sum(own * own, axis=1), "member", axis=0, tiled=True
-            )
+            everyone = lax.all_to_all(
+                jnp.broadcast_to(block[None], (members,) + block.shape),
+                "member",
+                split_axis=0,
+                concat_axis=0,
+                tiled=True,
+            ).reshape(K, features + 128)
+            prototype_lowbits = everyone[:, :features]
+            parts = everyone[:, features : features + 3].astype(jnp.float32)
+            half_quadratic_length = (parts[:, 0] + parts[:, 1]) + parts[:, 2]
     prototype_position_cost = smoothing_scale * closing_log_partition
     returned = lax.all_to_all(
         prototype_position_cost, ("group", "member"), split_axis=0, concat_axis=0, tiled=True

time: 217 us -> 176 us (0.81)
  between operations: 15 us -> 0.96 us
  waiting for transfers between devices: 95.1 us -> 86.9 us
  blocking collectives: 29.5 us -> 22.3 us
  local copies, waits for them, and re-layouts: 23 us -> 16.3 us
  starting transfers between devices: 29 us -> 25.3 us
    unnamed x1 -> x0, blocking collectives: 29.5 us -> none
    all_to_all x0 -> x1, blocking collectives: none -> 22.3 us  [shards(): lax.all_to_all(jnp.broadcast_to(block[None], (members,) + block.shape), '...]
    all_gather x1 -> x0, waiting for transfers between devices: 8.16 us -> none  [shards(): lax.all_gather(own.astype(jnp.bfloat16), 'member', axis=0, tiled=True)]
    gather x1 -> x0, local copies, waits for them, and re-layouts: 4.07 us -> none  [shards(): unit_rows[jnp.maximum(source, 0)]]
    all_to_all x1, starting transfers between devices: 9.25 us -> 5.46 us  [shards(): lax.all_to_all(prototype_position_cost, ('group', 'member'), split_axis=0...]
    dot_general x0 -> x1, matrix products: none -> 2.78 us  [shards(): jnp.dot(placement, unit_rows, preferred_element_type=jnp.float32)]
    scatter x1 -> x0, local copies, waits for them, and re-layouts: 2.44 us -> none  [shards(): source = jnp.full((clusters * capacity,), -1, jnp.int32).at[slot_of].set(...]
    select_n x2 -> x1, other arithmetic: 2.26 us -> 0.01 us  [shards(): row_energy = returned[slot_of]]
  transfers between devices with their start and end apart: 5 -> 4, of which waited for: 5 -> 4; matrix products, arithmetic and copies ran while one was open for 5% -> 6% of each run, Pallas kernels for 0% -> 0%
where the time goes in v2:
time: 176 us; the launch traced here: 175 us
  waiting for transfers between devices  86.9 us (49%)
  starting transfers between devices  25.3 us (14%)
  blocking collectives  22.3 us (13%)
  local copies, waits for them, and re-layouts  16.3 us (9%)
  other arithmetic  13 us (7%)
  matrix products  10.6 us (6%)
    all_to_all x2, waiting for transfers between devices, shards(): lax.all_to_all(combined, 'member', split_axis=0, concat_axis=0, tiled=True)  55.4 us
    all_to_all x1, waiting for transfers between devices, shards(): lax.all_to_all(packed, ('group', 'member'), split_axis=0, concat_axis=0,...  29.4 us
    all_to_all x1, blocking collectives, shards(): lax.all_to_all(jnp.broadcast_to(block[None], (members,) + block.shape), '...  22.3 us
    all_to_all x1, starting transfers between devices, shards(): lax.all_to_all(packed, ('group', 'member'), split_axis=0, concat_axis=0,...  11.5 us
    all_to_all x2, starting transfers between devices, shards(): lax.all_to_all(combined, 'member', split_axis=0, concat_axis=0, tiled=True)  8.38 us
    all_to_all x2, local copies, waits for them, and re-layouts, shards(): lax.all_to_all(combined, 'member', split_axis=0, concat_axis=0, tiled=True)  5.59 us
    all_to_all x1, starting transfers between devices, shards(): lax.all_to_all(prototype_position_cost, ('group', 'member'), split_axis=0...  5.46 us
    dot_general x2, matrix products, shards(): jnp.einsum('rk,rd->kd', weights, arrived, preferred_element_type=jnp.floa...  5.24 us
  transfers between devices with their start and end apart: 4, of which 4 were waited for; matrix products, arithmetic and copies ran while one was open for 6% of the time, Pallas kernels for 0%

profile of v2, /device:TPU:1, one launch (start us, length us, event | category | flops | bytes accessed | tf_op | source)
XLA Modules:
  0.0 175.5 jit_solution(7632794737493172324)
XLA Ops:
  0.7 0.9 copy.27
  1.5 0.2 fusion.18
  1.8 0.9 fusion.17
  2.8 0.7 multiply_add_fusion
  3.4 0.3 convert_reduce_fusion.2
  3.8 0.3 fusion
  4.1 2.8 %select_bitcast_fusion = bf16[128,8,1024]{2,1,0:T(8,128)(2,1)} fusion(pred[1024]{0:T(1024)(128)(4,1)S(1)} %broadcast_compare_fusion, bf16[512,1024]{1,0:T(8,128)(2,1)S(1)} %copy-done.3, bf16[1024]{0:T(1024)(128)(2,1)S(1)} %fusion.21, f32[512]{0:T(512)S(1)} %add_rsqrt_fusion, s32[512]{0:T(512)S(1)} %multiply_add_fusion), kind=kOutput, calls=%fused_computation.18 | convolution fusion | flops 1078460416 | bytes 3152896 | tf_op jit(solution)/shard_map/dot_general | solution.py:44
  6.8 11.5 %all-to-all-start = ((bf16[128,8,1024]{2,1,0:T(8,128)(2,1)}), bf16[128,8,1024]{2,1,0:T(8,128)(2,1)S(1)}, u32[]{:S(2)}, u32[]{:S(2)}) async-start(bf16[128,8,1024]{2,1,0:T(8,128)(2,1)} %select_bitcast_fusion), calls=%async_computation | async-start | bytes 4194304 | tf_op jit(solution)/shard_map/all_to_all | solution.py:48
  18.3 0.3 multiply_reduce_fusion
  18.6 29.4 %all-to-all-done = bf16[128,8,1024]{2,1,0:T(8,128)(2,1)S(1)} async-done(((bf16[128,8,1024]{2,1,0:T(8,128)(2,1)}), bf16[128,8,1024]{2,1,0:T(8,128)(2,1)S(1)}, u32[]{:S(2)}, u32[]{:S(2)}) %all-to-all-start) | async-done | bytes 2097184 | tf_op jit(solution)/shard_map/all_to_all | solution.py:48
  48.0 0.2 convert_reduce_fusion.3
  48.2 1.3 fusion.5
  49.5 0.5 fusion.7
  50.0 0.8 convert_reduce_fusion.1
  50.8 2.6 %fusion.28 = f32[512,1024]{1,0:T(8,128)} fusion(bf16[1024,512]{0,1:T(8,128)(2,1)S(1)} %get-tuple-element.7, bf16[128,8,1024]{2,1,0:T(8,128)(2,1)S(1)} %all-to-all-done), kind=kOutput, calls=%fused_computation.74 | convolution fusion | flops 1073741824 | bytes 5242880 | tf_op jit(solution)/shard_map/rk,rd->kd/dot_general | solution.py:65
  53.4 1.7 reshape.163
  55.2 0.1 select_maximum_fusion.1
  55.4 2.8 %all_to_all.32 = f32[16,1,32896]{2,1,0:T(1,128)} reshape(f32[16,32896]{1,0:T(8,128)S(1)} %select_maximum_fusion.1) | data formatting | bytes 4210688 | tf_op jit(solution)/shard_map/all_to_all | solution.py:75
  58.2 3.7 %all-to-all-start.1 = ((f32[16,1,32896]{2,1,0:T(1,128)}), f32[16,1,32896]{2,1,0:T(1,128)S(1)}, u32[]{:S(2)}, u32[]{:S(2)}) async-start(f32[16,1,32896]{2,1,0:T(1,128)} %all_to_all.32), calls=%async_computation.1 | async-start | bytes 4210688 | tf_op jit(solution)/shard_map/all_to_all | solution.py:75
  61.9 1.6 convert_element_type.60
  63.5 28.1 %all-to-all-done.1 = f32[16,1,32896]{2,1,0:T(1,128)S(1)} async-done(((f32[16,1,32896]{2,1,0:T(1,128)}), f32[16,1,32896]{2,1,0:T(1,128)S(1)}, u32[]{:S(2)}, u32[]{:S(2)}) %all-to-all-start.1) | async-done | bytes 2105376 | tf_op jit(solution)/shard_map/all_to_all | solution.py:75
  91.6 1.3 reduce_sum.107
  93.0 0.3 slice_reduce_fusion.1
  93.4 1.1 multiply_reduce_fusion.1
  94.5 0.1 copy.29
  94.6 0.1 copy.30
  94.7 0.1 copy.31
  94.8 0.1 concatenate.11
  95.0 22.3 %all_to_all.44 = bf16[16,32,1152]{2,1,0:T(8,128)(2,1)S(1)} all-to-all(bf16[16,32,1152]{2,1,0:T(8,128)(2,1)S(1)} %broadcast_in_dim.38), channel_id=1, replica_groups=mesh['group'=8,'member'=16] {'member'}, dimensions={0} | all-to-all | bytes 2359296 | tf_op jit(solution)/shard_map/all_to_all | solution.py:96
  117.4 0.3 fusion.15
  117.7 1.3 fusion.6
  119.0 0.5 fusion.8
  119.5 0.8 convert_reduce_fusion
  120.3 0.7 mul.136
  121.1 5.5 %all-to-all-start.4 = ((f32[128,8,1]{1,2,0:T(1,128)}), f32[128,8,1]{1,2,0:T(1,128)S(1)}, u32[]{:S(2)}, u32[]{:S(2)}) async-start(f32[128,8,1]{1,2,0:T(1,128)} %bitcast.11), calls=%async_computation.4 | async-start | bytes 131072 | tf_op jit(solution)/shard_map/all_to_all | solution.py:107
  126.5 2.6 %fusion.25 = f32[512,1024]{1,0:T(8,128)} fusion(bf16[1024,512]{0,1:T(8,128)(2,1)S(1)} %get-tuple-element.3, bf16[128,8,1024]{2,1,0:T(8,128)(2,1)S(1)} %copy-done.2), kind=kOutput, calls=%fused_computation.71 | convolution fusion | flops 1073741824 | bytes 5242880 | tf_op jit(solution)/shard_map/rk,rd->kd/dot_general | solution.py:65
  129.1 1.7 reshape.166
  131.0 0.1 select_maximum_fusion
  131.1 2.8 %all_to_all.35 = f32[16,1,32896]{2,1,0:T(1,128)} reshape(f32[16,32896]{1,0:T(8,128)S(1)} %select_maximum_fusion) | data formatting | bytes 4210688 | tf_op jit(solution)/shard_map/all_to_all | solution.py:75
  133.9 2.1 %all-to-all-done.4 = f32[128,8,1]{1,2,0:T(1,128)S(1)} async-done(((f32[128,8,1]{1,2,0:T(1,128)}), f32[128,8,1]{1,2,0:T(1,128)S(1)}, u32[]{:S(2)}, u32[]{:S(2)}) %all-to-all-start.4) | async-done | bytes 4128 | tf_op jit(solution)/shard_map/all_to_all | solution.py:107
  136.1 4.7 %all-to-all-start.3 = ((f32[16,1,32896]{2,1,0:T(1,128)}), f32[16,1,32896]{2,1,0:T(1,128)S(1)}, u32[]{:S(2)}, u32[]{:S(2)}) async-start(f32[16,1,32896]{2,1,0:T(1,128)} %all_to_all.35), calls=%async_computation.3 | async-start | bytes 4210688 | tf_op jit(solution)/shard_map/all_to_all | solution.py:75
  140.8 0.5 broadcast.151
  141.3 0.8 reduce.17
  142.2 3.4 %gather_fusion = f32[512]{0:T(512)} fusion(f32[1024]{0:T(1024)S(1)} %all_to_all.38, s32[1024]{0:T(1024)S(1)} %pad_clamp_fusion), kind=kCustom, calls=%fused_computation | custom fusion | bytes 6144 | tf_op jit(solution)/shard_map/gather | solution.py:110
  145.6 27.3 %all-to-all-done.3 = f32[16,1,32896]{2,1,0:T(1,128)S(1)} async-done(((f32[16,1,32896]{2,1,0:T(1,128)}), f32[16,1,32896]{2,1,0:T(1,128)S(1)}, u32[]{:S(2)}, u32[]{:S(2)}) %all-to-all-start.3) | async-done | bytes 2105376 | tf_op jit(solution)/shard_map/all_to_all | solution.py:75
  172.9 1.3 reduce_sum.111
  174.3 0.3 slice_reduce_fusion
  174.7 0.7 add_divide_fusion
  (37 shorter events, 0.8 us)
Async XLA Ops:
  0.6 3.1 %copy-start.3 = (bf16[512,1024]{1,0:T(8,128)(2,1)S(1)}, bf16[512,1024]{1,0:T(8,128)(2,1)}, u32[]{:S(2)}) copy-start(bf16[512,1024]{1,0:T(8,128)(2,1)} %param.3) | copy-start | bytes 3145732
  6.8 11.5 %copy-start = (bf16[512,1024]{1,0:T(8,128)(2,1)S(1)}, bf16[512,1024]{1,0:T(8,128)(2,1)}, u32[]{:S(2)}) copy-start(bf16[512,1024]{1,0:T(8,128)(2,1)} %param.5) | copy-start | bytes 3145732
  6.8 41.2 %all-to-all-start = ((bf16[128,8,1024]{2,1,0:T(8,128)(2,1)}), bf16[128,8,1024]{2,1,0:T(8,128)(2,1)S(1)}, u32[]{:S(2)}, u32[]{:S(2)}) async-start(bf16[128,8,1024]{2,1,0:T(8,128)(2,1)} %select_bitcast_fusion), calls=%async_computation | async-start | bytes 4194304 | tf_op jit(solution)/shard_map/all_to_all | solution.py:48
  48.0 2.8 %copy-start.1 = (bf16[128,8,1024]{2,1,0:T(8,128)(2,1)}, bf16[128,8,1024]{2,1,0:T(8,128)(2,1)S(1)}, u32[]{:S(2)}) copy-start(bf16[128,8,1024]{2,1,0:T(8,128)(2,1)S(1)} %all-to-all-done) | copy-start | bytes 6291460
  58.2 33.4 %all-to-all-start.1 = ((f32[16,1,32896]{2,1,0:T(1,128)}), f32[16,1,32896]{2,1,0:T(1,128)S(1)}, u32[]{:S(2)}, u32[]{:S(2)}) async-start(f32[16,1,32896]{2,1,0:T(1,128)} %all_to_all.32), calls=%async_computation.1 | async-start | bytes 4210688 | tf_op jit(solution)/shard_map/all_to_all | solution.py:75
  94.9 22.8 %copy-start.2 = (bf16[128,8,1024]{2,1,0:T(8,128)(2,1)S(1)}, bf16[128,8,1024]{2,1,0:T(8,128)(2,1)}, u32[]{:S(2)}) copy-start(bf16[128,8,1024]{2,1,0:T(8,128)(2,1)} %copy-done.1) | copy-start | bytes 6291460
  121.1 15.0 %all-to-all-start.4 = ((f32[128,8,1]{1,2,0:T(1,128)}), f32[128,8,1]{1,2,0:T(1,128)S(1)}, u32[]{:S(2)}, u32[]{:S(2)}) async-start(f32[128,8,1]{1,2,0:T(1,128)} %bitcast.11), calls=%async_computation.4 | async-start | bytes 131072 | tf_op jit(solution)/shard_map/all_to_all | solution.py:107
  133.9 6.8 %copy-start.4 = (s32[512,1]{0,1:T(1,128)S(1)}, s32[512,1]{0,1:T(1,128)}, u32[]{:S(2)}) copy-start(s32[512,1]{0,1:T(1,128)} %param.4) | copy-start | bytes 6148
  136.1 36.9 %all-to-all-start.3 = ((f32[16,1,32896]{2,1,0:T(1,128)}), f32[16,1,32896]{2,1,0:T(1,128)S(1)}, u32[]{:S(2)}, u32[]{:S(2)}) async-start(f32[16,1,32896]{2,1,0:T(1,128)} %all_to_all.35), calls=%async_computation.3 | async-start | bytes 4210688 | tf_op jit(solution)/shard_map/all_to_all | solution.py:75

commit v3 on v2

--- a/solution.py
+++ b/solution.py
@@ -65,19 +65,13 @@
         weighted = jnp.einsum("rk,rd->kd", weights, arrived, preferred_element_type=jnp.float32)
         masses = jnp.sum(weights.astype(jnp.float32), axis=0)
         combined = jnp.concatenate(
-            [
-                weighted.reshape(members, share_rows * features),
-                jnp.pad(masses.reshape(members, share_rows), ((0, 0), (0, 128 - share_rows))),
-            ],
-            axis=1,
+            [weighted, masses[:, None], jnp.zeros((K, 127), jnp.float32)], axis=1
+        ).reshape(members, share_rows, features + 128)
+        reduced = jnp.sum(
+            lax.all_to_all(combined, "member", split_axis=0, concat_axis=0, tiled=True), axis=0
         )
-        reduced = jnp.sum(
-            lax.all_to_all(combined, "member", split_axis=0, concat_axis=0, tiled=True),
-            axis=0,
-            keepdims=True,
-        )
-        weighted_own = reduced[0, : share_rows * features].reshape(share_rows, features)
-        masses_own = reduced[0, share_rows * features : share_rows * features + share_rows]
+        weighted_own = reduced[:, :features]
+        masses_own = reduced[:, features]
         own = (weighted_own + prior_mass * own) / (masses_own + prior_mass)[:, None]
         if iteration + 1 < ITERS:
             half_own = 0.5 * jnp.sum(own * own, axis=1)

time: 176 us -> 182 us (1.034)
  waiting for transfers between devices: 86.9 us -> 94.4 us
  local copies, waits for them, and re-layouts: 16.3 us -> 14.3 us
    concatenate x0 -> x5, local copies, waits for them, and re-layouts: none -> 8.08 us  [shards(): jnp.concatenate([weighted, masses[:, None], jnp.zeros((K, 127), jnp.float...]
    all_to_all x2, waiting for transfers between devices: 55.4 us -> 62.1 us  [shards(): lax.all_to_all(combined, 'member', split_axis=0, concat_axis=0, tiled=True)]
    all_to_all x2 -> x0, local copies, waits for them, and re-layouts: 5.59 us -> none  [shards(): lax.all_to_all(combined, 'member', split_axis=0, concat_axis=0, tiled=True)]
    reshape x4 -> x0, local copies, waits for them, and re-layouts: 3.64 us -> none  [the longest x2 3.49 us: shards(): weighted.reshape(members, share_rows * features)]
    reduce_sum x2, other arithmetic: 2.62 us -> 0.24 us  [shards(): jnp.sum(lax.all_to_all(combined, 'member', split_axis=0, concat_axis=0, t...]
  transfers between devices with their start and end apart: 4 -> 4, of which waited for: 4 -> 4; matrix products, arithmetic and copies ran while one was open for 6% -> 8% of each run, Pallas kernels for 0% -> 0%
where the time goes in v3:
time: 182 us; the launch traced here: 181 us
  waiting for transfers between devices  94.4 us (52%)
  starting transfers between devices  25.8 us (14%)
  blocking collectives  21.7 us (12%)
  local copies, waits for them, and re-layouts  14.3 us (8%)
  other arithmetic  12.3 us (7%)
  matrix products  11.8 us (6%)
    all_to_all x2, waiting for transfers between devices, shards(): lax.all_to_all(combined, 'member', split_axis=0, concat_axis=0, tiled=True)  62.1 us
    all_to_all x1, waiting for transfers between devices, shards(): lax.all_to_all(packed, ('group', 'member'), split_axis=0, concat_axis=0,...  29.4 us
    all_to_all x1, blocking collectives, shards(): lax.all_to_all(jnp.broadcast_to(block[None], (members,) + block.shape), '...  21.7 us
    all_to_all x1, starting transfers between devices, shards(): lax.all_to_all(packed, ('group', 'member'), split_axis=0, concat_axis=0,...  11.5 us
    concatenate x5, local copies, waits for them, and re-layouts, shards(): jnp.concatenate([weighted, masses[:, None], jnp.zeros((K, 127), jnp.float...  8.08 us
    all_to_all x2, starting transfers between devices, shards(): lax.all_to_all(combined, 'member', split_axis=0, concat_axis=0, tiled=True)  7.71 us
    all_to_all x1, starting transfers between devices, shards(): lax.all_to_all(prototype_position_cost, ('group', 'member'), split_axis=0...  6.61 us
    dot_general x2, matrix products, shards(): jnp.einsum('rk,rd->kd', weights, arrived, preferred_element_type=jnp.floa...  6.41 us
  transfers between devices with their start and end apart: 4, of which 4 were waited for; matrix products, arithmetic and copies ran while one was open for 8% of the time, Pallas kernels for 0%

profile of v3, /device:TPU:1, one launch (start us, length us, event | category | flops | bytes accessed | tf_op | source)
XLA Modules:
  0.0 181.2 jit_solution(1460415954128425429)
XLA Ops:
  0.7 0.9 copy.32
  1.5 0.2 fusion.22
  1.8 0.9 fusion.21
  2.8 0.7 multiply_add_fusion
  3.4 0.3 convert_reduce_fusion.2
  3.8 0.3 fusion
  4.1 2.8 %select_bitcast_fusion = bf16[128,8,1024]{2,1,0:T(8,128)(2,1)} fusion(pred[1024]{0:T(1024)(128)(4,1)S(1)} %broadcast_compare_fusion, bf16[512,1024]{1,0:T(8,128)(2,1)S(1)} %copy-done.5, bf16[1024]{0:T(1024)(128)(2,1)S(1)} %fusion.29, f32[512]{0:T(512)S(1)} %add_rsqrt_fusion, s32[512]{0:T(512)S(1)} %multiply_add_fusion), kind=kOutput, calls=%fused_computation.19 | convolution fusion | flops 1078460416 | bytes 3152896 | tf_op jit(solution)/shard_map/dot_general | solution.py:44
  6.8 11.5 %all-to-all-start = ((bf16[128,8,1024]{2,1,0:T(8,128)(2,1)}), bf16[128,8,1024]{2,1,0:T(8,128)(2,1)S(1)}, u32[]{:S(2)}, u32[]{:S(2)}) async-start(bf16[128,8,1024]{2,1,0:T(8,128)(2,1)} %select_bitcast_fusion), calls=%async_computation | async-start | bytes 4194304 | tf_op jit(solution)/shard_map/all_to_all | solution.py:48
  18.3 0.3 multiply_reduce_fusion
  18.6 29.4 %all-to-all-done = bf16[128,8,1024]{2,1,0:T(8,128)(2,1)S(1)} async-done(((bf16[128,8,1024]{2,1,0:T(8,128)(2,1)}), bf16[128,8,1024]{2,1,0:T(8,128)(2,1)S(1)}, u32[]{:S(2)}, u32[]{:S(2)}) %all-to-all-start) | async-done | bytes 2097184 | tf_op jit(solution)/shard_map/all_to_all | solution.py:48
  48.0 0.2 convert_reduce_fusion.3
  48.2 1.3 fusion.9
  49.5 0.5 fusion.11
  50.0 1.7 convert_reduce_fusion.1
  51.7 0.2 concatenate.24
  51.9 3.8 %fusion.5 = f32[16,32,1024]{2,1,0:T(8,128)} fusion(bf16[16,32,1024]{2,1,0:T(8,128)(2,1)} %bitcast.58, bf16[128,8,1024]{2,1,0:T(8,128)(2,1)S(1)} %all-to-all-done), kind=kOutput, calls=%fused_computation.8 | convolution fusion | flops 1073741824 | bytes 5242880 | tf_op jit(solution)/shard_map/rk,rd->kd/dot_general | solution.py:65
  55.8 3.9 %concatenate.20 = f32[16,32,1152]{2,1,0:T(8,128)} concatenate(f32[16,32,1024]{2,1,0:T(8,128)} %fusion.5, f32[16,32,1]{2,1,0:T(8,128)S(1)} %concatenate.24, f32[16,32,127]{2,1,0:T(8,128)S(1)} %concatenate.19), dimensions={2} | concatenate | bytes 4718592 | tf_op jit(solution)/shard_map/concatenate | solution.py:67
  59.6 3.7 %all-to-all-start.1 = ((f32[16,32,1152]{2,1,0:T(8,128)}), f32[16,32,1152]{2,1,0:T(8,128)S(1)}, u32[]{:S(2)}, u32[]{:S(2)}) async-start(f32[16,32,1152]{2,1,0:T(8,128)} %concatenate.20), calls=%async_computation.1 | async-start | bytes 4718592 | tf_op jit(solution)/shard_map/all_to_all | solution.py:71
  63.4 1.6 convert_element_type.63
  65.0 31.9 %all-to-all-done.1 = f32[16,32,1152]{2,1,0:T(8,128)S(1)} async-done(((f32[16,32,1152]{2,1,0:T(8,128)}), f32[16,32,1152]{2,1,0:T(8,128)S(1)}, u32[]{:S(2)}, u32[]{:S(2)}) %all-to-all-start.1) | async-done | bytes 2359328 | tf_op jit(solution)/shard_map/all_to_all | solution.py:71
  96.8 0.1 reduce_sum.107
  96.9 0.1 fusion.28
  97.0 1.1 multiply_reduce_fusion.1
  98.2 0.1 copy.35
  98.3 0.1 copy.36
  98.4 0.1 copy.37
  98.5 0.1 concatenate.21
  98.6 0.1 broadcast_in_dim.33
  98.7 21.7 %all_to_all.36 = bf16[16,32,1152]{2,1,0:T(8,128)(2,1)S(1)} all-to-all(bf16[16,32,1152]{2,1,0:T(8,128)(2,1)S(1)} %broadcast_in_dim.33), channel_id=1, replica_groups=mesh['group'=8,'member'=16] {'member'}, dimensions={0} | all-to-all | bytes 2359296 | tf_op jit(solution)/shard_map/all_to_all | solution.py:90
  120.4 0.3 fusion.19
  120.7 1.3 fusion.10
  122.0 0.5 fusion.12
  122.5 0.8 convert_reduce_fusion
  123.3 0.7 mul.147
  124.1 6.6 %all-to-all-start.4 = ((f32[128,8,1]{1,2,0:T(1,128)}), f32[128,8,1]{1,2,0:T(1,128)}, u32[]{:S(2)}, u32[]{:S(2)}) async-start(f32[128,8,1]{1,2,0:T(1,128)} %bitcast.14), calls=%async_computation.4 | async-start | bytes 131072 | tf_op jit(solution)/shard_map/all_to_all | solution.py:101
  130.7 2.6 %fusion.3 = f32[16,32,1024]{2,1,0:T(8,128)} fusion(bf16[16,32,1024]{2,1,0:T(8,128)(2,1)S(1)} %bitcast.57, bf16[128,8,1024]{2,1,0:T(8,128)(2,1)S(1)} %copy-done.2), kind=kOutput, calls=%fused_computation.6 | convolution fusion | flops 1073741824 | bytes 5242880 | tf_op jit(solution)/shard_map/rk,rd->kd/dot_general | solution.py:65
  133.3 0.2 concatenate.25
  133.5 3.8 %concatenate.23 = f32[16,32,1152]{2,1,0:T(8,128)} concatenate(f32[16,32,1024]{2,1,0:T(8,128)} %fusion.3, f32[16,32,1]{2,1,0:T(8,128)S(1)} %concatenate.25, f32[16,32,127]{2,1,0:T(8,128)S(1)} %copy-done.4), dimensions={2} | concatenate | bytes 4718592 | tf_op jit(solution)/shard_map/concatenate | solution.py:67
  137.3 3.0 %all-to-all-done.4 = f32[128,8,1]{1,2,0:T(1,128)} async-done(((f32[128,8,1]{1,2,0:T(1,128)}), f32[128,8,1]{1,2,0:T(1,128)}, u32[]{:S(2)}, u32[]{:S(2)}) %all-to-all-start.4) | async-done | bytes 4128 | tf_op jit(solution)/shard_map/all_to_all | solution.py:101
  140.2 4.0 %all-to-all-start.3 = ((f32[16,32,1152]{2,1,0:T(8,128)}), f32[16,32,1152]{2,1,0:T(8,128)S(1)}, u32[]{:S(2)}, u32[]{:S(2)}) async-start(f32[16,32,1152]{2,1,0:T(8,128)} %concatenate.23), calls=%async_computation.3 | async-start | bytes 4718592 | tf_op jit(solution)/shard_map/all_to_all | solution.py:71
  144.3 0.5 broadcast.154
  144.8 1.7 reduce.11
  146.4 0.1 all_to_all.30
  146.5 3.4 %gather_fusion = f32[512]{0:T(512)} fusion(f32[1024]{0:T(1024)S(1)} %all_to_all.30, s32[1024]{0:T(1024)S(1)} %pad_clamp_fusion), kind=kCustom, calls=%fused_computation | custom fusion | bytes 6144 | tf_op jit(solution)/shard_map/gather | solution.py:104
  150.0 30.2 %all-to-all-done.3 = f32[16,32,1152]{2,1,0:T(8,128)S(1)} async-done(((f32[16,32,1152]{2,1,0:T(8,128)}), f32[16,32,1152]{2,1,0:T(8,128)S(1)}, u32[]{:S(2)}, u32[]{:S(2)}) %all-to-all-start.3) | async-done | bytes 2359328 | tf_op jit(solution)/shard_map/all_to_all | solution.py:71
  180.2 0.1 reduce_sum.111
  180.3 0.1 fusion.27
  180.4 0.7 fusion.24
  (32 shorter events, 0.2 us)
Async XLA Ops:
  0.6 3.1 %copy-start.5 = (bf16[512,1024]{1,0:T(8,128)(2,1)S(1)}, bf16[512,1024]{1,0:T(8,128)(2,1)}, u32[]{:S(2)}) copy-start(bf16[512,1024]{1,0:T(8,128)(2,1)} %param.3) | copy-start | bytes 3145732
  6.8 11.5 %copy-start = (bf16[512,1024]{1,0:T(8,128)(2,1)S(1)}, bf16[512,1024]{1,0:T(8,128)(2,1)}, u32[]{:S(2)}) copy-start(bf16[512,1024]{1,0:T(8,128)(2,1)} %param.5) | copy-start | bytes 3145732
  6.8 41.2 %all-to-all-start = ((bf16[128,8,1024]{2,1,0:T(8,128)(2,1)}), bf16[128,8,1024]{2,1,0:T(8,128)(2,1)S(1)}, u32[]{:S(2)}, u32[]{:S(2)}) async-start(bf16[128,8,1024]{2,1,0:T(8,128)(2,1)} %select_bitcast_fusion), calls=%async_computation | async-start | bytes 4194304 | tf_op jit(solution)/shard_map/all_to_all | solution.py:48
  48.0 3.9 %copy-start.1 = (bf16[128,8,1024]{2,1,0:T(8,128)(2,1)}, bf16[128,8,1024]{2,1,0:T(8,128)(2,1)S(1)}, u32[]{:S(2)}) copy-start(bf16[128,8,1024]{2,1,0:T(8,128)(2,1)S(1)} %all-to-all-done) | copy-start | bytes 6291460
  55.7 3.9 %copy-start.3 = (f32[16,32,127]{2,1,0:T(8,128)}, f32[16,32,127]{2,1,0:T(8,128)S(1)}, u32[]{:S(2)}) copy-start(f32[16,32,127]{2,1,0:T(8,128)S(1)} %concatenate.19) | copy-start | bytes 780292
  59.6 37.2 %all-to-all-start.1 = ((f32[16,32,1152]{2,1,0:T(8,128)}), f32[16,32,1152]{2,1,0:T(8,128)S(1)}, u32[]{:S(2)}, u32[]{:S(2)}) async-start(f32[16,32,1152]{2,1,0:T(8,128)} %concatenate.20), calls=%async_computation.1 | async-start | bytes 4718592 | tf_op jit(solution)/shard_map/all_to_all | solution.py:71
  98.6 22.1 %copy-start.2 = (bf16[128,8,1024]{2,1,0:T(8,128)(2,1)S(1)}, bf16[128,8,1024]{2,1,0:T(8,128)(2,1)}, u32[]{:S(2)}) copy-start(bf16[128,8,1024]{2,1,0:T(8,128)(2,1)} %copy-done.1) | copy-start | bytes 6291460
  124.1 16.2 %all-to-all-start.4 = ((f32[128,8,1]{1,2,0:T(1,128)}), f32[128,8,1]{1,2,0:T(1,128)}, u32[]{:S(2)}, u32[]{:S(2)}) async-start(f32[128,8,1]{1,2,0:T(1,128)} %bitcast.14), calls=%async_computation.4 | async-start | bytes 131072 | tf_op jit(solution)/shard_map/all_to_all | solution.py:101
  130.7 2.8 %copy-start.4 = (f32[16,32,127]{2,1,0:T(8,128)S(1)}, f32[16,32,127]{2,1,0:T(8,128)}, u32[]{:S(2)}) copy-start(f32[16,32,127]{2,1,0:T(8,128)} %copy-done.3) | copy-start | bytes 780292
  137.3 7.0 %copy-start.6 = (s32[512,1]{0,1:T(1,128)S(1)}, s32[512,1]{0,1:T(1,128)}, u32[]{:S(2)}) copy-start(s32[512,1]{0,1:T(1,128)} %param.4) | copy-start | bytes 6148
  140.2 40.0 %all-to-all-start.3 = ((f32[16,32,1152]{2,1,0:T(8,128)}), f32[16,32,1152]{2,1,0:T(8,128)S(1)}, u32[]{:S(2)}, u32[]{:S(2)}) async-start(f32[16,32,1152]{2,1,0:T(8,128)} %concatenate.23), calls=%async_computation.3 | async-start | bytes 4718592 | tf_op jit(solution)/shard_map/all_to_all | solution.py:71

commit v4 on v2

--- a/solution.py
+++ b/solution.py
@@ -3,6 +3,7 @@
 import jax
 import jax.numpy as jnp
 from jax import lax
+from jax.sharding import Mesh
 from jax.sharding import PartitionSpec as P
 
 K = 512
@@ -13,15 +14,25 @@
 prior_mass = 32.0
 empty_mark = 2.0
 
+ALL = ("z", "core", "yhi", "ylo", "x")
+ROUTE = ("z", "yhi", "core", "ylo", "x")
+TEAM = ("core", "ylo", "x")
+PLANE = ("ylo", "x")
+
 
 def shards(embeddings, coarse_ids, centroid_seeds):
     rows_dev, features = embeddings.shape
-    groups = lax.axis_size("group")
-    members = lax.axis_size("member")
-    clusters = groups * members
+    cores = lax.axis_size("core")
+    plane = lax.axis_size("ylo") * lax.axis_size("x")
+    members = cores * plane
+    clusters = members * lax.axis_size("z") * lax.axis_size("yhi")
     capacity = 2 * rows_dev // clusters
     share_rows = K // members
-    first_row = lax.axis_index("member") * share_rows
+    core = lax.axis_index("core")
+    yhi = lax.axis_index("yhi")
+    first_row = lax.axis_index(TEAM) * share_rows
+    partner = lax.ppermute(centroid_seeds, "core", [(0, 1), (1, 0)])
+    seeds16 = jnp.where(core == yhi, centroid_seeds, partner)
     widened = embeddings.astype(jnp.float32)
     unit_rows = (
         widened
@@ -45,11 +56,11 @@
         jnp.bfloat16
     )
     packed = jnp.where(filled[:, None], gathered, empty_row[None, :])
-    arrived = lax.all_to_all(packed, ("group", "member"), split_axis=0, concat_axis=0, tiled=True)
+    arrived = lax.all_to_all(packed, ROUTE, split_axis=0, concat_axis=0, tiled=True)
     slot_mask = (arrived[:, 0].astype(jnp.float32) < 1.5).astype(jnp.float32)
-    seeds = centroid_seeds.astype(jnp.float32)
+    seeds = seeds16.astype(jnp.float32)
     own = lax.dynamic_slice_in_dim(seeds, first_row, share_rows, 0)
-    prototype_lowbits = centroid_seeds
+    prototype_lowbits = seeds16
     half_quadratic_length = 0.5 * jnp.sum(seeds * seeds, axis=1)
     closing_log_partition = jnp.zeros((clusters * capacity,), jnp.float32)
     for iteration in range(ITERS):
@@ -71,8 +82,16 @@
             ],
             axis=1,
         )
+        width = combined.shape[1]
+        halves = jnp.sum(
+            lax.all_to_all(
+                combined.reshape(cores, plane, width), "core", split_axis=0, concat_axis=0,
+                tiled=True,
+            ),
+            axis=0,
+        )
         reduced = jnp.sum(
-            lax.all_to_all(combined, "member", split_axis=0, concat_axis=0, tiled=True),
+            lax.all_to_all(halves, PLANE, split_axis=0, concat_axis=0, tiled=True),
             axis=0,
             keepdims=True,
         )
@@ -93,9 +112,16 @@
                 ],
                 axis=1,
             )
+            on_plane = lax.all_to_all(
+                jnp.broadcast_to(block[None], (plane,) + block.shape),
+                PLANE,
+                split_axis=0,
+                concat_axis=0,
+                tiled=True,
+            )
             everyone = lax.all_to_all(
-                jnp.broadcast_to(block[None], (members,) + block.shape),
-                "member",
+                jnp.broadcast_to(on_plane[None], (cores,) + on_plane.shape),
+                "core",
                 split_axis=0,
                 concat_axis=0,
                 tiled=True,
@@ -105,13 +131,16 @@
             half_quadratic_length = (parts[:, 0] + parts[:, 1]) + parts[:, 2]
     prototype_position_cost = smoothing_scale * closing_log_partition
     returned = lax.all_to_all(
-        prototype_position_cost, ("group", "member"), split_axis=0, concat_axis=0, tiled=True
+        prototype_position_cost, ROUTE, split_axis=0, concat_axis=0, tiled=True
     )
     row_energy = returned[slot_of]
-    return (own, row_energy)
+    refined = lax.ppermute(own, ("core", "yhi"), [(0, 0), (1, 2), (2, 1), (3, 3)])
+    return (refined, row_energy)
 
 
 def solution(mesh):
-    in_specs = (P(("group", "member"), None), P(("group", "member"), None), P("group", None))
-    out_specs = (P(("group", "member"), None), P(("group", "member")))
-    return jax.shard_map(shards, mesh=mesh, in_specs=in_specs, out_specs=out_specs, check_vma=False)
+    groups, members = mesh.devices.shape
+    fine = Mesh(mesh.devices.reshape(groups // 2, 2, 2, members // 8, 4), ALL)
+    in_specs = (P(ALL, None), P(ALL, None), P(("z", "core"), None))
+    out_specs = (P(ALL, None), P(ALL))
+    return jax.shard_map(shards, mesh=fine, in_specs=in_specs, out_specs=out_specs, check_vma=False)

time: 176 us -> 165 us (0.938)
  waiting for transfers between devices: 86.9 us -> 67.6 us
  blocking collectives: 22.3 us -> 30.4 us
  starting transfers between devices: 25.3 us -> 27.2 us
    all_to_all x4, waiting for transfers between devices: 86.9 us -> 65.1 us  [the longest x2 31.7 us: shards(): lax.all_to_all(halves, PLANE, split_axis=0, concat_axis=0, tiled=True)]
    all_to_all x1 -> x4, blocking collectives: 22.3 us -> 30.4 us  [the longest x1 12 us: shards(): lax.all_to_all(jnp.broadcast_to(block[None], (plane,) + block.shape), PLA...]
    ppermute x0 -> x2, starting transfers between devices: none -> 4.02 us  [the longest x1 2.87 us: shards(): lax.ppermute(own, ('core', 'yhi'), [(0, 0), (1, 2), (2, 1), (3, 3)])]
    concatenate x0 -> x4, local copies, waits for them, and re-layouts: none -> 3.51 us  [shards(): jnp.concatenate([weighted.reshape(members, share_rows * features), jnp.pa...]
    reshape x2 -> x0, local copies, waits for them, and re-layouts: 3.49 us -> none  [shards(): weighted.reshape(members, share_rows * features)]
    ppermute x0 -> x2, waiting for transfers between devices: none -> 2.42 us  [the longest x1 2.42 us: shards(): partner = lax.ppermute(centroid_seeds, 'core', [(0, 1), (1, 0)])]
    all_to_all x4, local copies, waits for them, and re-layouts: 6.2 us -> 4.01 us  [the longest x2 3.41 us: shards(): lax.all_to_all(halves, PLANE, split_axis=0, concat_axis=0, tiled=True)]
    all_to_all x4, starting transfers between devices: 25.3 us -> 23.2 us  [the longest x1 11.5 us: shards(): lax.all_to_all(packed, ROUTE, split_axis=0, concat_axis=0, tiled=True)]
  transfers between devices with their start and end apart: 4 -> 6, of which waited for: 4 -> 5; matrix products, arithmetic and copies ran while one was open for 6% -> 5% of each run, Pallas kernels for 0% -> 0%
where the time goes in v4:
time: 165 us
  waiting for transfers between devices  67.6 us (41%)
  blocking collectives  30.4 us (18%)
  starting transfers between devices  27.2 us (16%)
  local copies, waits for them, and re-layouts  14.9 us (9%)
  other arithmetic  13 us (8%)
  matrix products  10.5 us (6%)
    all_to_all x2, waiting for transfers between devices, shards(): lax.all_to_all(halves, PLANE, split_axis=0, concat_axis=0, tiled=True)  31.7 us
    all_to_all x1, waiting for transfers between devices, shards(): lax.all_to_all(packed, ROUTE, split_axis=0, concat_axis=0, tiled=True)  23.7 us
    all_to_all x1, blocking collectives, shards(): lax.all_to_all(jnp.broadcast_to(block[None], (plane,) + block.shape), PLA...  12 us
    all_to_all x2, blocking collectives, shards(): lax.all_to_all(combined.reshape(cores, plane, width), 'core', split_axis=...  11.6 us
    all_to_all x1, starting transfers between devices, shards(): lax.all_to_all(packed, ROUTE, split_axis=0, concat_axis=0, tiled=True)  11.5 us
    all_to_all x1, waiting for transfers between devices, shards(): lax.all_to_all(prototype_position_cost, ROUTE, split_axis=0, concat_axis=...  9.8 us
    all_to_all x2, starting transfers between devices, shards(): lax.all_to_all(halves, PLANE, split_axis=0, concat_axis=0, tiled=True)  7.11 us
    all_to_all x1, blocking collectives, shards(): lax.all_to_all(jnp.broadcast_to(on_plane[None], (cores,) + on_plane.shape...  6.7 us
  transfers between devices with their start and end apart: 6, of which 5 were waited for; matrix products, arithmetic and copies ran while one was open for 5% of the time, Pallas kernels for 0%

profile of v4, /device:TPU:1, one launch (start us, length us, event | category | flops | bytes accessed | tf_op | source)
XLA Modules:
  0.0 164.5 jit_solution(2142109210980677881)
XLA Ops:
  0.7 0.9 copy.27
  1.8 0.9 fusion.17
  2.8 0.7 multiply_add_fusion
  3.4 0.3 convert_reduce_fusion.2
  3.8 0.3 fusion
  4.1 2.7 %select_bitcast_fusion = bf16[128,8,1024]{2,1,0:T(8,128)(2,1)} fusion(pred[1024]{0:T(1024)(128)(4,1)S(1)} %broadcast_compare_fusion, bf16[512,1024]{1,0:T(8,128)(2,1)S(1)} %copy-done.2, bf16[1024]{0:T(1024)(128)(2,1)S(1)} %fusion.21, f32[512]{0:T(512)S(1)} %add_rsqrt_fusion, s32[512]{0:T(512)S(1)} %multiply_add_fusion), kind=kOutput, calls=%fused_computation.17 | convolution fusion | flops 1078460416 | bytes 3152896 | tf_op jit(solution)/shard_map/dot_general | solution.py:55
  6.8 11.5 %all-to-all-start = ((bf16[128,8,1024]{2,1,0:T(8,128)(2,1)}), bf16[128,8,1024]{2,1,0:T(8,128)(2,1)S(1)}, u32[]{:S(2)}, u32[]{:S(2)}) async-start(bf16[128,8,1024]{2,1,0:T(8,128)(2,1)} %select_bitcast_fusion), calls=%async_computation | async-start | bytes 4194304 | tf_op jit(solution)/shard_map/all_to_all | solution.py:59
  18.3 1.1 collective-permute-start
  19.4 2.4 %collective-permute-done = bf16[512,1024]{1,0:T(8,128)(2,1)} collective-permute-done((bf16[512,1024]{1,0:T(8,128)(2,1)S(1)}, bf16[512,1024]{1,0:T(8,128)(2,1)}, u32[]{:S(2)}, u32[]{:S(2)}) %collective-permute-start) | collective-permute-done | bytes 1048608 | tf_op jit(solution)/shard_map/ppermute | solution.py:34
  21.9 2.8 %fusion.33 = (f32[512,1024]{1,0:T(8,128)}, bf16[512,1024]{1,0:T(8,128)(2,1)S(1)}) fusion(bf16[512,1024]{1,0:T(8,128)(2,1)} %param.5, bf16[512,1024]{1,0:T(8,128)(2,1)} %collective-permute-done, pred[]{:T(512)S(6)} %eq.61), kind=kLoop, calls=%fused_computation.81 | loop fusion | flops 1048576 | bytes 5242881 | tf_op jit(solution)/shard_map/convert_element_type | solution.py:61
  24.6 0.3 multiply_reduce_fusion
  24.9 23.7 %all-to-all-done = bf16[128,8,1024]{2,1,0:T(8,128)(2,1)S(1)} async-done(((bf16[128,8,1024]{2,1,0:T(8,128)(2,1)}), bf16[128,8,1024]{2,1,0:T(8,128)(2,1)S(1)}, u32[]{:S(2)}, u32[]{:S(2)}) %all-to-all-start) | async-done | bytes 2097184 | tf_op jit(solution)/shard_map/all_to_all | solution.py:59
  48.7 1.3 fusion.5
  50.0 0.5 fusion.7
  50.5 0.8 convert_reduce_fusion.1
  51.4 2.6 %fusion.28 = f32[512,1024]{1,0:T(8,128)} fusion(bf16[1024,512]{0,1:T(8,128)(2,1)S(1)} %get-tuple-element.9, bf16[128,8,1024]{2,1,0:T(8,128)(2,1)S(1)} %all-to-all-done), kind=kOutput, calls=%fused_computation.76 | convolution fusion | flops 1073741824 | bytes 5242880 | tf_op jit(solution)/shard_map/rk,rd->kd/dot_general | solution.py:76
  54.0 1.7 %concatenate.20 = f32[2,8,32768]{2,1,0:T(8,128)S(1)} reshape(f32[512,1024]{1,0:T(8,128)} %fusion.28) | data formatting | bytes 4194304 | tf_op jit(solution)/shard_map/concatenate | solution.py:78
  55.9 6.3 %all_to_all.59 = f32[2,8,32896]{2,1,0:T(8,128)S(1)} all-to-all(f32[2,8,32896]{2,1,0:T(8,128)S(1)} %pad_maximum_fusion), channel_id=1, replica_groups=mesh['z'=4,'core'=2,'yhi'=2,'ylo'=2,'x'=4] {'core'}, dimensions={0} | all-to-all | bytes 4210688 | tf_op jit(solution)/shard_map/all_to_all | solution.py:87
  62.2 0.3 reduce_sum.125
  62.5 1.7 %all_to_all.42 = f32[8,1,32896]{2,1,0:T(1,128)} reshape(f32[8,32896]{1,0:T(8,128)S(1)} %reduce_sum.125) | data formatting | bytes 2105344 | tf_op jit(solution)/shard_map/all_to_all | solution.py:94
  64.2 3.6 %all-to-all-start.2 = ((f32[8,1,32896]{2,1,0:T(1,128)}), f32[8,1,32896]{2,1,0:T(1,128)S(1)}, u32[]{:S(2)}, u32[]{:S(2)}) async-start(f32[8,1,32896]{2,1,0:T(1,128)} %all_to_all.42), calls=%async_computation.2 | async-start | bytes 2105344 | tf_op jit(solution)/shard_map/all_to_all | solution.py:94
  67.8 15.8 %all-to-all-done.2 = f32[8,1,32896]{2,1,0:T(1,128)S(1)} async-done(((f32[8,1,32896]{2,1,0:T(1,128)}), f32[8,1,32896]{2,1,0:T(1,128)S(1)}, u32[]{:S(2)}, u32[]{:S(2)}) %all-to-all-start.2) | async-done | bytes 1052704 | tf_op jit(solution)/shard_map/all_to_all | solution.py:94
  83.6 0.8 reduce_sum.126
  84.5 0.3 slice_reduce_fusion.1
  84.9 1.1 multiply_reduce_fusion.1
  86.5 12.0 %all_to_all.60 = bf16[8,32,1152]{2,1,0:T(8,128)(2,1)S(1)} all-to-all(bf16[8,32,1152]{2,1,0:T(8,128)(2,1)S(1)} %broadcast_in_dim.40), channel_id=1, replica_groups=mesh['z'=4,'core'=2,'yhi'=2,'ylo'=2,'x'=4] {'ylo','x'}, dimensions={0} | all-to-all | bytes 1179648 | tf_op jit(solution)/shard_map/all_to_all | solution.py:115
  98.6 6.7 %all_to_all.61 = bf16[2,8,32,1152]{3,2,1,0:T(8,128)(2,1)S(1)} all-to-all(bf16[2,8,32,1152]{3,2,1,0:T(8,128)(2,1)S(1)} %broadcast_in_dim.41), channel_id=1, replica_groups=mesh['z'=4,'core'=2,'yhi'=2,'ylo'=2,'x'=4] {'core'}, dimensions={0} | all-to-all | bytes 2359296 | tf_op jit(solution)/shard_map/all_to_all | solution.py:122
  105.4 0.3 fusion.15
  105.7 1.3 fusion.6
  107.0 0.5 fusion.8
  107.5 0.8 convert_reduce_fusion
  108.3 2.6 %fusion.25 = f32[512,1024]{1,0:T(8,128)} fusion(bf16[1024,512]{0,1:T(8,128)(2,1)S(1)} %get-tuple-element.3, bf16[128,8,1024]{2,1,0:T(8,128)(2,1)S(1)} %copy-done.1), kind=kOutput, calls=%fused_computation.73 | convolution fusion | flops 1073741824 | bytes 5242880 | tf_op jit(solution)/shard_map/rk,rd->kd/dot_general | solution.py:76
  110.9 1.7 %concatenate.24 = f32[2,8,32768]{2,1,0:T(8,128)S(1)} reshape(f32[512,1024]{1,0:T(8,128)} %fusion.25) | data formatting | bytes 4194304 | tf_op jit(solution)/shard_map/concatenate | solution.py:78
  112.9 5.3 %all_to_all.62 = f32[2,8,32896]{2,1,0:T(8,128)S(1)} all-to-all(f32[2,8,32896]{2,1,0:T(8,128)S(1)} %pad_maximum_fusion.1), channel_id=1, replica_groups=mesh['z'=4,'core'=2,'yhi'=2,'ylo'=2,'x'=4] {'core'}, dimensions={0} | all-to-all | bytes 4210688 | tf_op jit(solution)/shard_map/all_to_all | solution.py:87
  118.2 0.3 reduce_sum.130
  118.5 1.7 %all_to_all.47 = f32[8,1,32896]{2,1,0:T(1,128)} reshape(f32[8,32896]{1,0:T(8,128)S(1)} %reduce_sum.130) | data formatting | bytes 2105344 | tf_op jit(solution)/shard_map/all_to_all | solution.py:94
  120.2 3.6 %all-to-all-start.6 = ((f32[8,1,32896]{2,1,0:T(1,128)}), f32[8,1,32896]{2,1,0:T(1,128)S(1)}, u32[]{:S(2)}, u32[]{:S(2)}) async-start(f32[8,1,32896]{2,1,0:T(1,128)} %all_to_all.47), calls=%async_computation.6 | async-start | bytes 2105344 | tf_op jit(solution)/shard_map/all_to_all | solution.py:94
  123.8 15.8 %all-to-all-done.6 = f32[8,1,32896]{2,1,0:T(1,128)S(1)} async-done(((f32[8,1,32896]{2,1,0:T(1,128)}), f32[8,1,32896]{2,1,0:T(1,128)S(1)}, u32[]{:S(2)}, u32[]{:S(2)}) %all-to-all-start.6) | async-done | bytes 1052704 | tf_op jit(solution)/shard_map/all_to_all | solution.py:94
  139.6 0.8 reduce_sum.131
  140.5 0.4 slice_reduce_fusion
  141.0 2.9 %collective-permute-start.1 = (f32[32,1024]{1,0:T(8,128)S(1)}, f32[32,1024]{1,0:T(8,128)S(1)}, u32[]{:S(2)}, u32[]{:S(2)}) collective-permute-start(f32[32,1024]{1,0:T(8,128)S(1)} %add_divide_fusion), channel_id=1, source_target_pairs={{0,0},{8,16},{16,8},{24,24},{1,1},{9,17},{17,9},{25,25},{2,2},{10,... | collective-permute-start | bytes 393224 | tf_op jit(solution)/shard_map/ppermute | solution.py:137
  143.9 0.7 mul.144
  144.6 4.6 %all-to-all-start.7 = ((f32[128,8,1]{1,2,0:T(1,128)}), f32[128,8,1]{1,2,0:T(1,128)S(1)}, u32[]{:S(2)}, u32[]{:S(2)}) async-start(f32[128,8,1]{1,2,0:T(1,128)} %bitcast.13), calls=%async_computation.7 | async-start | bytes 131072 | tf_op jit(solution)/shard_map/all_to_all | solution.py:133
  149.2 9.8 %all-to-all-done.7 = f32[128,8,1]{1,2,0:T(1,128)S(1)} async-done(((f32[128,8,1]{1,2,0:T(1,128)}), f32[128,8,1]{1,2,0:T(1,128)S(1)}, u32[]{:S(2)}, u32[]{:S(2)}) %all-to-all-start.7) | async-done | bytes 4128 | tf_op jit(solution)/shard_map/all_to_all | solution.py:133
  159.0 0.5 broadcast.144
  159.5 0.8 reduce.17
  160.4 3.4 %gather_fusion = f32[512]{0:T(512)} fusion(f32[1024]{0:T(1024)S(1)} %all_to_all.50, s32[1024]{0:T(1024)S(1)} %pad_clamp_fusion), kind=kCustom, calls=%fused_computation | custom fusion | bytes 6144 | tf_op jit(solution)/shard_map/gather | solution.py:136
  163.9 0.7 copy.34
  (50 shorter events, 2.0 us)
Async XLA Ops:
  0.6 3.1 %copy-start.2 = (bf16[512,1024]{1,0:T(8,128)(2,1)S(1)}, bf16[512,1024]{1,0:T(8,128)(2,1)}, u32[]{:S(2)}) copy-start(bf16[512,1024]{1,0:T(8,128)(2,1)} %param.3) | copy-start | bytes 3145732
  6.8 11.5 %copy-start.3 = (bf16[512,1024]{1,0:T(8,128)(2,1)S(1)}, bf16[512,1024]{1,0:T(8,128)(2,1)}, u32[]{:S(2)}) copy-start(bf16[512,1024]{1,0:T(8,128)(2,1)} %param.5) | copy-start | bytes 3145732
  6.8 41.8 %all-to-all-start = ((bf16[128,8,1024]{2,1,0:T(8,128)(2,1)}), bf16[128,8,1024]{2,1,0:T(8,128)(2,1)S(1)}, u32[]{:S(2)}, u32[]{:S(2)}) async-start(bf16[128,8,1024]{2,1,0:T(8,128)(2,1)} %select_bitcast_fusion), calls=%async_computation | async-start | bytes 4194304 | tf_op jit(solution)/shard_map/all_to_all | solution.py:59
  18.3 3.6 %collective-permute-start = (bf16[512,1024]{1,0:T(8,128)(2,1)S(1)}, bf16[512,1024]{1,0:T(8,128)(2,1)}, u32[]{:S(2)}, u32[]{:S(2)}) collective-permute-start(bf16[512,1024]{1,0:T(8,128)(2,1)S(1)} %copy-done.3), channel_id=1, source_target_pairs={{0,16},{16,0},{1,17},{17,1},{2,18},{18,2},{3,19},{19,3},{4,20},{20... | collective-permute-start | bytes 3145736 | tf_op jit(solution)/shard_map/ppermute | solution.py:34
  48.6 2.8 %copy-start = (bf16[128,8,1024]{2,1,0:T(8,128)(2,1)}, bf16[128,8,1024]{2,1,0:T(8,128)(2,1)S(1)}, u32[]{:S(2)}) copy-start(bf16[128,8,1024]{2,1,0:T(8,128)(2,1)S(1)} %all-to-all-done) | copy-start | bytes 6291460
  64.2 19.4 %all-to-all-start.2 = ((f32[8,1,32896]{2,1,0:T(1,128)}), f32[8,1,32896]{2,1,0:T(1,128)S(1)}, u32[]{:S(2)}, u32[]{:S(2)}) async-start(f32[8,1,32896]{2,1,0:T(1,128)} %all_to_all.42), calls=%async_computation.2 | async-start | bytes 2105344 | tf_op jit(solution)/shard_map/all_to_all | solution.py:94
  98.6 7.0 %copy-start.1 = (bf16[128,8,1024]{2,1,0:T(8,128)(2,1)S(1)}, bf16[128,8,1024]{2,1,0:T(8,128)(2,1)}, u32[]{:S(2)}) copy-start(bf16[128,8,1024]{2,1,0:T(8,128)(2,1)} %copy-done) | copy-start | bytes 6291460
  118.5 5.3 %copy-start.4 = (s32[512,1]{0,1:T(1,128)S(1)}, s32[512,1]{0,1:T(1,128)}, u32[]{:S(2)}) copy-start(s32[512,1]{0,1:T(1,128)} %param.4) | copy-start | bytes 6148
  120.2 19.4 %all-to-all-start.6 = ((f32[8,1,32896]{2,1,0:T(1,128)}), f32[8,1,32896]{2,1,0:T(1,128)S(1)}, u32[]{:S(2)}, u32[]{:S(2)}) async-start(f32[8,1,32896]{2,1,0:T(1,128)} %all_to_all.47), calls=%async_computation.6 | async-start | bytes 2105344 | tf_op jit(solution)/shard_map/all_to_all | solution.py:94
  141.0 22.9 %collective-permute-start.1 = (f32[32,1024]{1,0:T(8,128)S(1)}, f32[32,1024]{1,0:T(8,128)S(1)}, u32[]{:S(2)}, u32[]{:S(2)}) collective-permute-start(f32[32,1024]{1,0:T(8,128)S(1)} %add_divide_fusion), channel_id=1, source_target_pairs={{0,0},{8,16},{16,8},{24,24},{1,1},{9,17},{17,9},{25,25},{2,2},{10,... | collective-permute-start | bytes 393224 | tf_op jit(solution)/shard_map/ppermute | solution.py:137
  144.6 14.4 %all-to-all-start.7 = ((f32[128,8,1]{1,2,0:T(1,128)}), f32[128,8,1]{1,2,0:T(1,128)S(1)}, u32[]{:S(2)}, u32[]{:S(2)}) async-start(f32[128,8,1]{1,2,0:T(1,128)} %bitcast.13), calls=%async_computation.7 | async-start | bytes 131072 | tf_op jit(solution)/shard_map/all_to_all | solution.py:133

commit v5 on v4

--- a/solution.py
+++ b/solution.py
@@ -62,7 +62,6 @@
     own = lax.dynamic_slice_in_dim(seeds, first_row, share_rows, 0)
     prototype_lowbits = seeds16
     half_quadratic_length = 0.5 * jnp.sum(seeds * seeds, axis=1)
-    closing_log_partition = jnp.zeros((clusters * capacity,), jnp.float32)
     for iteration in range(ITERS):
         similarity_logits = (
             jnp.dot(arrived, prototype_lowbits.T, preferred_element_type=jnp.float32)
@@ -73,6 +72,11 @@
         row_sum = jnp.sum(powers, axis=1, keepdims=True)
         weights = (powers / row_sum * slot_mask[:, None]).astype(jnp.bfloat16)
         closing_log_partition = row_max[:, 0] + jnp.log(row_sum[:, 0])
+        if iteration + 1 == ITERS:
+            returned = lax.all_to_all(
+                smoothing_scale * closing_log_partition, ROUTE, split_axis=0, concat_axis=0,
+                tiled=True,
+            )
         weighted = jnp.einsum("rk,rd->kd", weights, arrived, preferred_element_type=jnp.float32)
         masses = jnp.sum(weights.astype(jnp.float32), axis=0)
         combined = jnp.concatenate(
@@ -83,13 +87,12 @@
             axis=1,
         )
         width = combined.shape[1]
-        halves = jnp.sum(
-            lax.all_to_all(
-                combined.reshape(cores, plane, width), "core", split_axis=0, concat_axis=0,
-                tiled=True,
-            ),
-            axis=0,
-        )
+        by_core = combined.reshape(cores, plane, width)
+        mine = lax.dynamic_index_in_dim(by_core, core, 0, keepdims=False)
+        theirs = lax.dynamic_index_in_dim(by_core, 1 - core, 0, keepdims=False)
+        halves = mine + lax.ppermute(theirs, "core", [(0, 1), (1, 0)])
+        if iteration + 1 == ITERS:
+            returned, halves = lax.optimization_barrier((returned, halves))
         reduced = jnp.sum(
             lax.all_to_all(halves, PLANE, split_axis=0, concat_axis=0, tiled=True),
             axis=0,
@@ -119,21 +122,19 @@
                 concat_axis=0,
                 tiled=True,
             )
-            everyone = lax.all_to_all(
-                jnp.broadcast_to(on_plane[None], (cores,) + on_plane.shape),
-                "core",
-                split_axis=0,
-                concat_axis=0,
-                tiled=True,
+            partner_plane = lax.ppermute(on_plane, "core", [(0, 1), (1, 0)])
+            everyone = jnp.concatenate(
+                [
+                    jnp.where(core == 0, on_plane, partner_plane),
+                    jnp.where(core == 0, partner_plane, on_plane),
+                ],
+                axis=0,
             ).reshape(K, features + 128)
             prototype_lowbits = everyone[:, :features]
             parts = everyone[:, features : features + 3].astype(jnp.float32)
             half_quadratic_length = (parts[:, 0] + parts[:, 1]) + parts[:, 2]
-    prototype_position_cost = smoothing_scale * closing_log_partition
-    returned = lax.all_to_all(
-        prototype_position_cost, ROUTE, split_axis=0, concat_axis=0, tiled=True
-    )
-    row_energy = returned[slot_of]
+    own_slot = slot_of[None, :] == jnp.arange(clusters * capacity, dtype=jnp.int32)[:, None]
+    row_energy = jnp.sum(jnp.where(own_slot, returned[:, None], 0.0), axis=0)
     refined = lax.ppermute(own, ("core", "yhi"), [(0, 0), (1, 2), (2, 1), (3, 3)])
     return (refined, row_energy)
 

time: 165 us -> 155 us (0.939)
  waiting for transfers between devices: 67.6 us -> 48.9 us
  blocking collectives: 30.4 us -> 43.3 us
  local copies, waits for them, and re-layouts: 14.9 us -> 10.9 us
  starting transfers between devices: 27.2 us -> 24 us
  other arithmetic: 13 us -> 15.6 us
    all_to_all x2 -> x1, waiting for transfers between devices: 31.7 us -> 15.8 us  [shards(): lax.all_to_all(halves, PLANE, split_axis=0, concat_axis=0, tiled=True)]
    all_to_all x3 -> x2, blocking collectives: 18.3 us -> 31.2 us  [the longest x1 18.3 us: shards(): lax.all_to_all(halves, PLANE, split_axis=0, concat_axis=0, tiled=True)]
    all_to_all x1 -> x0, waiting for transfers between devices: 9.8 us -> none  [shards(): lax.all_to_all(prototype_position_cost, ROUTE, split_axis=0, concat_axis=...]
    all_to_all x1 -> x0, starting transfers between devices: 4.59 us -> none  [shards(): lax.all_to_all(prototype_position_cost, ROUTE, split_axis=0, concat_axis=...]
    ppermute x0 -> x3, waiting for transfers between devices: none -> 4.14 us  [the longest x2 2.51 us: shards(): halves = mine + lax.ppermute(theirs, 'core', [(0, 1), (1, 0)])]
    ppermute x0 -> x3, starting transfers between devices: none -> 3.85 us  [the longest x1 2.21 us: shards(): partner_plane = lax.ppermute(on_plane, 'core', [(0, 1), (1, 0)])]
    all_to_all x2 -> x1, starting transfers between devices: 7.11 us -> 3.56 us  [shards(): lax.all_to_all(halves, PLANE, split_axis=0, concat_axis=0, tiled=True)]
    gather x1 -> x0, local copies, waits for them, and re-layouts: 3.42 us -> none  [shards(): row_energy = returned[slot_of]]
  transfers between devices with their start and end apart: 6 -> 7, of which waited for: 5 -> 6; matrix products, arithmetic and copies ran while one was open for 5% -> 3% of each run, Pallas kernels for 0% -> 0%
where the time goes in v5:
time: 155 us; the launch traced here: 154 us
  waiting for transfers between devices  48.9 us (32%)
  blocking collectives  43.3 us (28%)
  starting transfers between devices  24 us (15%)
  other arithmetic  15.6 us (10%)
  local copies, waits for them, and re-layouts  10.9 us (7%)
  matrix products  10.5 us (7%)
    all_to_all x1, waiting for transfers between devices, shards(): lax.all_to_all(packed, ROUTE, split_axis=0, concat_axis=0, tiled=True)  23.7 us
    all_to_all x1, blocking collectives, shards(): lax.all_to_all(halves, PLANE, split_axis=0, concat_axis=0, tiled=True)  18.3 us
    all_to_all x1, waiting for transfers between devices, shards(): lax.all_to_all(halves, PLANE, split_axis=0, concat_axis=0, tiled=True)  15.8 us
    all_to_all x1, blocking collectives, shards(): lax.all_to_all(smoothing_scale * closing_log_partition, ROUTE, split_axis...  12.9 us
    all_to_all x1, blocking collectives, shards(): lax.all_to_all(jnp.broadcast_to(block[None], (plane,) + block.shape), PLA...  12 us
    all_to_all x1, starting transfers between devices, shards(): lax.all_to_all(packed, ROUTE, split_axis=0, concat_axis=0, tiled=True)  11.5 us
    dot_general x2, matrix products, shards(): jnp.einsum('rk,rd->kd', weights, arrived, preferred_element_type=jnp.floa...  5.22 us
    ppermute x1, starting transfers between devices, shards(): lax.ppermute(own, ('core', 'yhi'), [(0, 0), (1, 2), (2, 1), (3, 3)])  3.98 us
  transfers between devices with their start and end apart: 7, of which 6 were waited for; matrix products, arithmetic and copies ran while one was open for 3% of the time, Pallas kernels for 0%

profile of v5, /device:TPU:1, one launch (start us, length us, event | category | flops | bytes accessed | tf_op | source)
XLA Modules:
  0.0 154.2 jit_solution(6109458168431854145)
XLA Ops:
  0.7 0.9 copy.27
  1.8 0.9 fusion.27
  2.8 0.7 multiply_add_fusion
  3.4 0.3 convert_reduce_fusion.2
  3.8 0.3 fusion
  4.1 2.7 %select_bitcast_fusion = bf16[128,8,1024]{2,1,0:T(8,128)(2,1)} fusion(pred[1024]{0:T(1024)(128)(4,1)S(1)} %broadcast_compare_fusion, bf16[512,1024]{1,0:T(8,128)(2,1)S(1)} %copy-done.2, bf16[1024]{0:T(1024)(128)(2,1)S(1)} %fusion.31, f32[512]{0:T(512)S(1)} %add_rsqrt_fusion, s32[512]{0:T(512)S(1)} %multiply_add_fusion), kind=kOutput, calls=%fused_computation.19 | convolution fusion | flops 1078460416 | bytes 3152896 | tf_op jit(solution)/shard_map/dot_general | solution.py:55
  6.8 11.5 %all-to-all-start = ((bf16[128,8,1024]{2,1,0:T(8,128)(2,1)}), bf16[128,8,1024]{2,1,0:T(8,128)(2,1)S(1)}, u32[]{:S(2)}, u32[]{:S(2)}) async-start(bf16[128,8,1024]{2,1,0:T(8,128)(2,1)} %select_bitcast_fusion), calls=%async_computation | async-start | bytes 4194304 | tf_op jit(solution)/shard_map/all_to_all | solution.py:59
  18.3 1.1 collective-permute-start
  19.4 2.4 %collective-permute-done = bf16[512,1024]{1,0:T(8,128)(2,1)} collective-permute-done((bf16[512,1024]{1,0:T(8,128)(2,1)S(1)}, bf16[512,1024]{1,0:T(8,128)(2,1)}, u32[]{:S(2)}, u32[]{:S(2)}) %collective-permute-start) | collective-permute-done | bytes 1048608 | tf_op jit(solution)/shard_map/ppermute | solution.py:34
  21.9 2.8 %fusion.43 = (f32[512,1024]{1,0:T(8,128)}, bf16[512,1024]{1,0:T(8,128)(2,1)S(1)}) fusion(bf16[512,1024]{1,0:T(8,128)(2,1)} %param.5, bf16[512,1024]{1,0:T(8,128)(2,1)} %collective-permute-done, pred[]{:T(512)S(6)} %eq.73), kind=kLoop, calls=%fused_computation.98 | loop fusion | flops 1048576 | bytes 5242881 | tf_op jit(solution)/shard_map/convert_element_type | solution.py:61
  24.9 23.7 %all-to-all-done = bf16[128,8,1024]{2,1,0:T(8,128)(2,1)S(1)} async-done(((bf16[128,8,1024]{2,1,0:T(8,128)(2,1)}), bf16[128,8,1024]{2,1,0:T(8,128)(2,1)S(1)}, u32[]{:S(2)}, u32[]{:S(2)}) %all-to-all-start) | async-done | bytes 2097184 | tf_op jit(solution)/shard_map/all_to_all | solution.py:59
  48.7 1.3 fusion.5
  50.0 0.5 fusion.7
  50.5 0.8 convert_reduce_fusion.1
  51.3 2.6 %fusion.38 = f32[512,1024]{1,0:T(8,128)} fusion(bf16[1024,512]{0,1:T(8,128)(2,1)S(1)} %get-tuple-element.13, bf16[128,8,1024]{2,1,0:T(8,128)(2,1)S(1)} %all-to-all-done), kind=kOutput, calls=%fused_computation.93 | convolution fusion | flops 1073741824 | bytes 5242880 | tf_op jit(solution)/shard_map/rk,rd->kd/dot_general | solution.py:80
  53.9 1.7 %concatenate.23 = f32[2,8,32768]{2,1,0:T(8,128)S(1)} reshape(f32[512,1024]{1,0:T(8,128)} %fusion.38) | data formatting | bytes 4194304 | tf_op jit(solution)/shard_map/concatenate | solution.py:82
  55.8 1.0 fusion.15
  56.8 1.3 collective-permute-start.1
  58.1 2.5 %collective-permute-done.1 = f32[8,32896]{1,0:T(8,128)S(1)} collective-permute-done((f32[8,32896]{1,0:T(8,128)}, f32[8,32896]{1,0:T(8,128)S(1)}, u32[]{:S(2)}, u32[]{:S(2)}) %collective-permute-start.1) | collective-permute-done | bytes 1052704 | tf_op jit(solution)/shard_map/ppermute | solution.py:93
  60.7 1.7 %all_to_all.32 = f32[8,1,32896]{2,1,0:T(1,128)} reshape(f32[8,32896]{1,0:T(8,128)S(1)} %fusion.18) | data formatting | bytes 2105344 | tf_op jit(solution)/shard_map/all_to_all | solution.py:97
  62.4 3.6 %all-to-all-start.1 = ((f32[8,1,32896]{2,1,0:T(1,128)}), f32[8,1,32896]{2,1,0:T(1,128)S(1)}, u32[]{:S(2)}, u32[]{:S(2)}) async-start(f32[8,1,32896]{2,1,0:T(1,128)} %all_to_all.32), calls=%async_computation.1 | async-start | bytes 2105344 | tf_op jit(solution)/shard_map/all_to_all | solution.py:97
  66.0 15.8 %all-to-all-done.1 = f32[8,1,32896]{2,1,0:T(1,128)S(1)} async-done(((f32[8,1,32896]{2,1,0:T(1,128)}), f32[8,1,32896]{2,1,0:T(1,128)S(1)}, u32[]{:S(2)}, u32[]{:S(2)}) %all-to-all-start.1) | async-done | bytes 1052704 | tf_op jit(solution)/shard_map/all_to_all | solution.py:97
  81.8 0.8 reduce_sum.114
  82.7 0.3 slice_reduce_fusion.1
  83.1 1.1 multiply_reduce_fusion.1
  84.7 12.0 %all_to_all.44 = bf16[8,32,1152]{2,1,0:T(8,128)(2,1)S(1)} all-to-all(bf16[8,32,1152]{2,1,0:T(8,128)(2,1)S(1)} %broadcast_in_dim.76), channel_id=1, replica_groups=mesh['z'=4,'core'=2,'yhi'=2,'ylo'=2,'x'=4] {'ylo','x'}, dimensions={0} | all-to-all | bytes 1179648 | tf_op jit(solution)/shard_map/all_to_all | solution.py:118
  96.7 2.2 %collective-permute-start.2 = (bf16[8,32,1152]{2,1,0:T(8,128)(2,1)S(1)}, bf16[8,32,1152]{2,1,0:T(8,128)(2,1)S(1)}, u32[]{:S(2)}, u32[]{:S(2)}) collective-permute-start(bf16[8,32,1152]{2,1,0:T(8,128)(2,1)S(1)} %all_to_all.44), channel_id=1, source_target_pairs={{0,16},{16,0},{1,17},{17,1},{2,18},{18,2},{3,19},{19,3},{4,20},{20... | collective-permute-start | bytes 1769480 | tf_op jit(solution)/shard_map/ppermute | solution.py:125
  99.0 1.6 %collective-permute-done.2 = bf16[8,32,1152]{2,1,0:T(8,128)(2,1)S(1)} collective-permute-done((bf16[8,32,1152]{2,1,0:T(8,128)(2,1)S(1)}, bf16[8,32,1152]{2,1,0:T(8,128)(2,1)S(1)}, u32[]{:S(2)}, u32[]{:S(2)}) %collective-permute-start.2) | collective-permute-done | bytes 589856 | tf_op jit(solution)/shard_map/ppermute | solution.py:125
  100.9 0.3 fusion.25
  101.2 1.1 copy-done.1
  102.3 1.3 fusion.6
  103.6 0.5 fusion.8
  104.1 0.8 convert_reduce_fusion
  104.9 2.6 %fusion.35 = f32[512,1024]{1,0:T(8,128)} fusion(bf16[1024,512]{0,1:T(8,128)(2,1)S(1)} %get-tuple-element.7, bf16[128,8,1024]{2,1,0:T(8,128)(2,1)S(1)} %copy-done.1), kind=kOutput, calls=%fused_computation.90 | convolution fusion | flops 1073741824 | bytes 5242880 | tf_op jit(solution)/shard_map/rk,rd->kd/dot_general | solution.py:80
  107.5 1.7 %concatenate.28 = f32[2,8,32768]{2,1,0:T(8,128)S(1)} reshape(f32[512,1024]{1,0:T(8,128)} %fusion.35) | data formatting | bytes 4194304 | tf_op jit(solution)/shard_map/concatenate | solution.py:82
  109.4 1.1 fusion.10
  110.4 0.4 collective-permute-start.3
  110.9 12.9 %all_to_all.45 = f32[128,8,1]{1,2,0:T(1,128)S(1)} all-to-all(f32[128,8,1]{1,2,0:T(1,128)S(1)} %bitcast.68), channel_id=1, replica_groups=mesh['z'=4,'core'=2,'yhi'=2,'ylo'=2,'x'=4] {'z','yhi','core','ylo','x'}, dimensions={0} | all-to-all | bytes 8192 | tf_op jit(solution)/shard_map/all_to_all | solution.py:76
  123.8 0.5 broadcast.137
  124.3 0.8 reduce.17
  125.4 0.7 all_to_all.37
  126.1 18.3 %all_to_all.46 = f32[8,1,32896]{2,1,0:T(1,128)S(1)} all-to-all(f32[8,1,32896]{2,1,0:T(1,128)S(1)} %all_to_all.37), channel_id=1, replica_groups=mesh['z'=4,'core'=2,'yhi'=2,'ylo'=2,'x'=4] {'ylo','x'}, dimensions={0} | all-to-all | bytes 2105344 | tf_op jit(solution)/shard_map/all_to_all | solution.py:97
  144.4 0.8 reduce_sum.118
  145.3 0.4 slice_reduce_fusion
  145.8 4.0 %collective-permute-start.4 = (f32[32,1024]{1,0:T(8,128)S(1)}, f32[32,1024]{1,0:T(8,128)S(1)}, u32[]{:S(2)}, u32[]{:S(2)}) collective-permute-start(f32[32,1024]{1,0:T(8,128)S(1)} %add_divide_fusion), channel_id=1, source_target_pairs={{0,0},{8,16},{16,8},{24,24},{1,1},{9,17},{17,9},{25,25},{2,2},{10,... | collective-permute-start | bytes 393224 | tf_op jit(solution)/shard_map/ppermute | solution.py:138
  149.8 0.9 select_reduce_fusion
  150.7 2.9 %collective-permute-done.4 = f32[32,1024]{1,0:T(8,128)S(1)} collective-permute-done((f32[32,1024]{1,0:T(8,128)S(1)}, f32[32,1024]{1,0:T(8,128)S(1)}, u32[]{:S(2)}, u32[]{:S(2)}) %collective-permute-start.4) | collective-permute-done | bytes 131104 | tf_op jit(solution)/shard_map/ppermute | solution.py:138
  153.6 0.7 copy.34
  (48 shorter events, 2.4 us)
Async XLA Ops:
  0.6 3.1 %copy-start.2 = (bf16[512,1024]{1,0:T(8,128)(2,1)S(1)}, bf16[512,1024]{1,0:T(8,128)(2,1)}, u32[]{:S(2)}) copy-start(bf16[512,1024]{1,0:T(8,128)(2,1)} %param.3) | copy-start | bytes 3145732
  6.8 11.5 %copy-start.3 = (bf16[512,1024]{1,0:T(8,128)(2,1)S(1)}, bf16[512,1024]{1,0:T(8,128)(2,1)}, u32[]{:S(2)}) copy-start(bf16[512,1024]{1,0:T(8,128)(2,1)} %param.5) | copy-start | bytes 3145732
  6.8 41.8 %all-to-all-start = ((bf16[128,8,1024]{2,1,0:T(8,128)(2,1)}), bf16[128,8,1024]{2,1,0:T(8,128)(2,1)S(1)}, u32[]{:S(2)}, u32[]{:S(2)}) async-start(bf16[128,8,1024]{2,1,0:T(8,128)(2,1)} %select_bitcast_fusion), calls=%async_computation | async-start | bytes 4194304 | tf_op jit(solution)/shard_map/all_to_all | solution.py:59
  18.3 3.6 %collective-permute-start = (bf16[512,1024]{1,0:T(8,128)(2,1)S(1)}, bf16[512,1024]{1,0:T(8,128)(2,1)}, u32[]{:S(2)}, u32[]{:S(2)}) collective-permute-start(bf16[512,1024]{1,0:T(8,128)(2,1)S(1)} %copy-done.3), channel_id=1, source_target_pairs={{0,16},{16,0},{1,17},{17,1},{2,18},{18,2},{3,19},{19,3},{4,20},{20... | collective-permute-start | bytes 3145736 | tf_op jit(solution)/shard_map/ppermute | solution.py:34
  48.6 2.8 %copy-start = (bf16[128,8,1024]{2,1,0:T(8,128)(2,1)}, bf16[128,8,1024]{2,1,0:T(8,128)(2,1)S(1)}, u32[]{:S(2)}) copy-start(bf16[128,8,1024]{2,1,0:T(8,128)(2,1)S(1)} %all-to-all-done) | copy-start | bytes 6291460
  56.8 3.8 %collective-permute-start.1 = (f32[8,32896]{1,0:T(8,128)}, f32[8,32896]{1,0:T(8,128)S(1)}, u32[]{:S(2)}, u32[]{:S(2)}) collective-permute-start(f32[8,32896]{1,0:T(8,128)} %fusion.15), channel_id=1, source_target_pairs={{0,16},{16,0},{1,17},{17,1},{2,18},{18,2},{3,19},{19,3},{4,20},{20... | collective-permute-start | bytes 3158024 | tf_op jit(solution)/shard_map/ppermute | solution.py:93
  62.4 19.4 %all-to-all-start.1 = ((f32[8,1,32896]{2,1,0:T(1,128)}), f32[8,1,32896]{2,1,0:T(1,128)S(1)}, u32[]{:S(2)}, u32[]{:S(2)}) async-start(f32[8,1,32896]{2,1,0:T(1,128)} %all_to_all.32), calls=%async_computation.1 | async-start | bytes 2105344 | tf_op jit(solution)/shard_map/all_to_all | solution.py:97
  96.7 3.8 %collective-permute-start.2 = (bf16[8,32,1152]{2,1,0:T(8,128)(2,1)S(1)}, bf16[8,32,1152]{2,1,0:T(8,128)(2,1)S(1)}, u32[]{:S(2)}, u32[]{:S(2)}) collective-permute-start(bf16[8,32,1152]{2,1,0:T(8,128)(2,1)S(1)} %all_to_all.44), channel_id=1, source_target_pairs={{0,16},{16,0},{1,17},{17,1},{2,18},{18,2},{3,19},{19,3},{4,20},{20... | collective-permute-start | bytes 1769480 | tf_op jit(solution)/shard_map/ppermute | solution.py:125
  100.7 1.6 %copy-start.1 = (bf16[128,8,1024]{2,1,0:T(8,128)(2,1)S(1)}, bf16[128,8,1024]{2,1,0:T(8,128)(2,1)}, u32[]{:S(2)}) copy-start(bf16[128,8,1024]{2,1,0:T(8,128)(2,1)} %copy-done) | copy-start | bytes 6291460
  110.4 14.8 %collective-permute-start.3 = (f32[8,32896]{1,0:T(8,128)}, f32[8,32896]{1,0:T(8,128)S(1)}, u32[]{:S(2)}, u32[]{:S(2)}) collective-permute-start(f32[8,32896]{1,0:T(8,128)} %fusion.10), channel_id=1, source_target_pairs={{0,16},{16,0},{1,17},{17,1},{2,18},{18,2},{3,19},{19,3},{4,20},{20... | collective-permute-start | bytes 3158024 | tf_op jit(solution)/shard_map/ppermute | solution.py:93
  145.8 7.8 %collective-permute-start.4 = (f32[32,1024]{1,0:T(8,128)S(1)}, f32[32,1024]{1,0:T(8,128)S(1)}, u32[]{:S(2)}, u32[]{:S(2)}) collective-permute-start(f32[32,1024]{1,0:T(8,128)S(1)} %add_divide_fusion), channel_id=1, source_target_pairs={{0,0},{8,16},{16,8},{24,24},{1,1},{9,17},{17,9},{25,25},{2,2},{10,... | collective-permute-start | bytes 393224 | tf_op jit(solution)/shard_map/ppermute | solution.py:138

commit v6 on v5

--- a/solution.py
+++ b/solution.py
@@ -73,10 +73,11 @@
         weights = (powers / row_sum * slot_mask[:, None]).astype(jnp.bfloat16)
         closing_log_partition = row_max[:, 0] + jnp.log(row_sum[:, 0])
         if iteration + 1 == ITERS:
+            energy = (smoothing_scale * closing_log_partition).reshape(-1, members, capacity)
+            energy = lax.all_to_all(energy, ("z", "yhi"), split_axis=0, concat_axis=0, tiled=True)
             returned = lax.all_to_all(
-                smoothing_scale * closing_log_partition, ROUTE, split_axis=0, concat_axis=0,
-                tiled=True,
-            )
+                energy, TEAM, split_axis=1, concat_axis=1, tiled=True
+            ).reshape(-1)
         weighted = jnp.einsum("rk,rd->kd", weights, arrived, preferred_element_type=jnp.float32)
         masses = jnp.sum(weights.astype(jnp.float32), axis=0)
         combined = jnp.concatenate(

time: 155 us -> 161 us (1.039)
  blocking collectives: 43.3 us -> 48.8 us
    all_to_all x1 -> x2, blocking collectives: 12.9 us -> 18.5 us  [the longest x1 9.62 us: shards(): lax.all_to_all(energy, TEAM, split_axis=1, concat_axis=1, tiled=True)]
  transfers between devices with their start and end apart: 7 -> 7, of which waited for: 6 -> 6; matrix products, arithmetic and copies ran while one was open for 3% -> 4% of each run, Pallas kernels for 0% -> 0%
where the time goes in v6:
time: 161 us; the launch traced here: 160 us
  waiting for transfers between devices  49.1 us (30%)
  blocking collectives  48.8 us (30%)
  starting transfers between devices  23.8 us (15%)
  other arithmetic  15.5 us (10%)
  local copies, waits for them, and re-layouts  11.2 us (7%)
  matrix products  10.5 us (7%)
    all_to_all x1, waiting for transfers between devices, shards(): lax.all_to_all(packed, ROUTE, split_axis=0, concat_axis=0, tiled=True)  23.7 us
    all_to_all x1, blocking collectives, shards(): lax.all_to_all(halves, PLANE, split_axis=0, concat_axis=0, tiled=True)  18.3 us
    all_to_all x1, waiting for transfers between devices, shards(): lax.all_to_all(halves, PLANE, split_axis=0, concat_axis=0, tiled=True)  15.8 us
    all_to_all x1, blocking collectives, shards(): lax.all_to_all(jnp.broadcast_to(block[None], (plane,) + block.shape), PLA...  12 us
    all_to_all x1, starting transfers between devices, shards(): lax.all_to_all(packed, ROUTE, split_axis=0, concat_axis=0, tiled=True)  11.5 us
    all_to_all x1, blocking collectives, shards(): lax.all_to_all(energy, TEAM, split_axis=1, concat_axis=1, tiled=True)  9.62 us
    all_to_all x1, blocking collectives, shards(): lax.all_to_all(energy, ('z', 'yhi'), split_axis=0, concat_axis=0, tiled=T...  8.9 us
    dot_general x2, matrix products, shards(): jnp.einsum('rk,rd->kd', weights, arrived, preferred_element_type=jnp.floa...  5.22 us
  transfers between devices with their start and end apart: 7, of which 6 were waited for; matrix products, arithmetic and copies ran while one was open for 4% of the time, Pallas kernels for 0%

profile of v6, /device:TPU:1, one launch (start us, length us, event | category | flops | bytes accessed | tf_op | source)
XLA Modules:
  0.0 160.0 jit_solution(4164386934845810786)
XLA Ops:
  0.7 0.9 copy.29
  1.8 0.9 fusion.27
  2.8 0.7 multiply_add_fusion
  3.4 0.3 convert_reduce_fusion.2
  4.1 2.7 %select_bitcast_fusion = bf16[128,8,1024]{2,1,0:T(8,128)(2,1)} fusion(pred[1024]{0:T(1024)(128)(4,1)S(1)} %broadcast_compare_fusion, bf16[512,1024]{1,0:T(8,128)(2,1)S(1)} %copy-done.2, bf16[1024]{0:T(1024)(128)(2,1)S(1)} %fusion.31, f32[512]{0:T(512)S(1)} %add_rsqrt_fusion, s32[512]{0:T(512)S(1)} %multiply_add_fusion), kind=kOutput, calls=%fused_computation.19 | convolution fusion | flops 1078460416 | bytes 3152896 | tf_op jit(solution)/shard_map/dot_general | solution.py:55
  6.8 11.5 %all-to-all-start = ((bf16[128,8,1024]{2,1,0:T(8,128)(2,1)}), bf16[128,8,1024]{2,1,0:T(8,128)(2,1)S(1)}, u32[]{:S(2)}, u32[]{:S(2)}) async-start(bf16[128,8,1024]{2,1,0:T(8,128)(2,1)} %select_bitcast_fusion), calls=%async_computation | async-start | bytes 4194304 | tf_op jit(solution)/shard_map/all_to_all | solution.py:59
  18.3 1.1 collective-permute-start
  19.4 2.4 %collective-permute-done = bf16[512,1024]{1,0:T(8,128)(2,1)} collective-permute-done((bf16[512,1024]{1,0:T(8,128)(2,1)S(1)}, bf16[512,1024]{1,0:T(8,128)(2,1)}, u32[]{:S(2)}, u32[]{:S(2)}) %collective-permute-start) | collective-permute-done | bytes 1048608 | tf_op jit(solution)/shard_map/ppermute | solution.py:34
  21.9 2.8 %fusion.43 = (f32[512,1024]{1,0:T(8,128)}, bf16[512,1024]{1,0:T(8,128)(2,1)S(1)}) fusion(bf16[512,1024]{1,0:T(8,128)(2,1)} %param.5, bf16[512,1024]{1,0:T(8,128)(2,1)} %collective-permute-done, pred[]{:T(512)S(6)} %eq.73), kind=kLoop, calls=%fused_computation.98 | loop fusion | flops 1048576 | bytes 5242881 | tf_op jit(solution)/shard_map/convert_element_type | solution.py:61
  24.9 23.7 %all-to-all-done = bf16[128,8,1024]{2,1,0:T(8,128)(2,1)S(1)} async-done(((bf16[128,8,1024]{2,1,0:T(8,128)(2,1)}), bf16[128,8,1024]{2,1,0:T(8,128)(2,1)S(1)}, u32[]{:S(2)}, u32[]{:S(2)}) %all-to-all-start) | async-done | bytes 2097184 | tf_op jit(solution)/shard_map/all_to_all | solution.py:59
  48.7 1.3 fusion.5
  50.0 0.5 fusion.7
  50.5 0.8 convert_reduce_fusion.1
  51.3 2.6 %fusion.38 = f32[512,1024]{1,0:T(8,128)} fusion(bf16[1024,512]{0,1:T(8,128)(2,1)S(1)} %get-tuple-element.13, bf16[128,8,1024]{2,1,0:T(8,128)(2,1)S(1)} %all-to-all-done), kind=kOutput, calls=%fused_computation.93 | convolution fusion | flops 1073741824 | bytes 5242880 | tf_op jit(solution)/shard_map/rk,rd->kd/dot_general | solution.py:81
  53.9 1.7 %concatenate.23 = f32[2,8,32768]{2,1,0:T(8,128)S(1)} reshape(f32[512,1024]{1,0:T(8,128)} %fusion.38) | data formatting | bytes 4194304 | tf_op jit(solution)/shard_map/concatenate | solution.py:83
  55.8 1.0 fusion.15
  56.8 1.3 collective-permute-start.1
  58.1 2.5 %collective-permute-done.1 = f32[8,32896]{1,0:T(8,128)S(1)} collective-permute-done((f32[8,32896]{1,0:T(8,128)}, f32[8,32896]{1,0:T(8,128)S(1)}, u32[]{:S(2)}, u32[]{:S(2)}) %collective-permute-start.1) | collective-permute-done | bytes 1052704 | tf_op jit(solution)/shard_map/ppermute | solution.py:94
  60.7 1.7 %all_to_all.32 = f32[8,1,32896]{2,1,0:T(1,128)} reshape(f32[8,32896]{1,0:T(8,128)S(1)} %fusion.18) | data formatting | bytes 2105344 | tf_op jit(solution)/shard_map/all_to_all | solution.py:98
  62.4 3.6 %all-to-all-start.1 = ((f32[8,1,32896]{2,1,0:T(1,128)}), f32[8,1,32896]{2,1,0:T(1,128)S(1)}, u32[]{:S(2)}, u32[]{:S(2)}) async-start(f32[8,1,32896]{2,1,0:T(1,128)} %all_to_all.32), calls=%async_computation.1 | async-start | bytes 2105344 | tf_op jit(solution)/shard_map/all_to_all | solution.py:98
  66.0 15.8 %all-to-all-done.1 = f32[8,1,32896]{2,1,0:T(1,128)S(1)} async-done(((f32[8,1,32896]{2,1,0:T(1,128)}), f32[8,1,32896]{2,1,0:T(1,128)S(1)}, u32[]{:S(2)}, u32[]{:S(2)}) %all-to-all-start.1) | async-done | bytes 1052704 | tf_op jit(solution)/shard_map/all_to_all | solution.py:98
  81.8 0.8 reduce_sum.114
  82.7 0.3 slice_reduce_fusion.1
  83.1 1.1 multiply_reduce_fusion.1
  84.7 12.0 %all_to_all.45 = bf16[8,32,1152]{2,1,0:T(8,128)(2,1)S(1)} all-to-all(bf16[8,32,1152]{2,1,0:T(8,128)(2,1)S(1)} %broadcast_in_dim.76), channel_id=1, replica_groups=mesh['z'=4,'core'=2,'yhi'=2,'ylo'=2,'x'=4] {'ylo','x'}, dimensions={0} | all-to-all | bytes 1179648 | tf_op jit(solution)/shard_map/all_to_all | solution.py:119
  96.7 2.2 %collective-permute-start.2 = (bf16[8,32,1152]{2,1,0:T(8,128)(2,1)S(1)}, bf16[8,32,1152]{2,1,0:T(8,128)(2,1)S(1)}, u32[]{:S(2)}, u32[]{:S(2)}) collective-permute-start(bf16[8,32,1152]{2,1,0:T(8,128)(2,1)S(1)} %all_to_all.45), channel_id=1, source_target_pairs={{0,16},{16,0},{1,17},{17,1},{2,18},{18,2},{3,19},{19,3},{4,20},{20... | collective-permute-start | bytes 1769480 | tf_op jit(solution)/shard_map/ppermute | solution.py:126
  99.0 1.6 %collective-permute-done.2 = bf16[8,32,1152]{2,1,0:T(8,128)(2,1)S(1)} collective-permute-done((bf16[8,32,1152]{2,1,0:T(8,128)(2,1)S(1)}, bf16[8,32,1152]{2,1,0:T(8,128)(2,1)S(1)}, u32[]{:S(2)}, u32[]{:S(2)}) %collective-permute-start.2) | collective-permute-done | bytes 589856 | tf_op jit(solution)/shard_map/ppermute | solution.py:126
  100.9 0.3 fusion.25
  101.2 1.1 copy-done.1
  102.3 1.3 fusion.6
  103.6 0.5 fusion.8
  104.1 0.8 convert_reduce_fusion
  104.9 2.6 %fusion.35 = f32[512,1024]{1,0:T(8,128)} fusion(bf16[1024,512]{0,1:T(8,128)(2,1)S(1)} %get-tuple-element.7, bf16[128,8,1024]{2,1,0:T(8,128)(2,1)S(1)} %copy-done.1), kind=kOutput, calls=%fused_computation.90 | convolution fusion | flops 1073741824 | bytes 5242880 | tf_op jit(solution)/shard_map/rk,rd->kd/dot_general | solution.py:81
  107.5 1.7 %concatenate.28 = f32[2,8,32768]{2,1,0:T(8,128)S(1)} reshape(f32[512,1024]{1,0:T(8,128)} %fusion.35) | data formatting | bytes 4194304 | tf_op jit(solution)/shard_map/concatenate | solution.py:83
  109.4 1.1 fusion.10
  110.4 0.4 collective-permute-start.3
  111.1 8.9 %all_to_all.46 = f32[8,1,128]{2,1,0:T(1,128)S(1)} all-to-all(f32[8,1,128]{2,1,0:T(1,128)S(1)} %reshape.167), channel_id=1, replica_groups=mesh['z'=4,'core'=2,'yhi'=2,'ylo'=2,'x'=4] {'z','yhi'}, dimensions={0} | all-to-all | bytes 8192 | tf_op jit(solution)/shard_map/all_to_all | solution.py:77
  120.0 0.5 broadcast.132
  120.5 0.7 reduce.14
  121.3 9.6 %all_to_all.47 = f32[8,16,8]{2,0,1:T(8,128)S(1)} all-to-all(f32[8,16,8]{2,0,1:T(8,128)S(1)} %copy.35), channel_id=1, replica_groups=mesh['z'=4,'core'=2,'yhi'=2,'ylo'=2,'x'=4] {'core','ylo','x'}, dimensions={1} | all-to-all | bytes 8192 | tf_op jit(solution)/shard_map/all_to_all | solution.py:78
  131.2 0.7 all_to_all.37
  131.9 18.3 %all_to_all.48 = f32[8,1,32896]{2,1,0:T(1,128)S(1)} all-to-all(f32[8,1,32896]{2,1,0:T(1,128)S(1)} %all_to_all.37), channel_id=1, replica_groups=mesh['z'=4,'core'=2,'yhi'=2,'ylo'=2,'x'=4] {'ylo','x'}, dimensions={0} | all-to-all | bytes 2105344 | tf_op jit(solution)/shard_map/all_to_all | solution.py:98
  150.2 0.8 reduce_sum.118
  151.1 0.4 slice_reduce_fusion
  151.6 3.8 %collective-permute-start.4 = (f32[32,1024]{1,0:T(8,128)S(1)}, f32[32,1024]{1,0:T(8,128)S(1)}, u32[]{:S(2)}, u32[]{:S(2)}) collective-permute-start(f32[32,1024]{1,0:T(8,128)S(1)} %add_divide_fusion), channel_id=1, source_target_pairs={{0,0},{8,16},{16,8},{24,24},{1,1},{9,17},{17,9},{25,25},{2,2},{10,... | collective-permute-start | bytes 393224 | tf_op jit(solution)/shard_map/ppermute | solution.py:139
  155.4 0.9 select_reduce_fusion
  156.3 3.1 %collective-permute-done.4 = f32[32,1024]{1,0:T(8,128)S(1)} collective-permute-done((f32[32,1024]{1,0:T(8,128)S(1)}, f32[32,1024]{1,0:T(8,128)S(1)}, u32[]{:S(2)}, u32[]{:S(2)}) %collective-permute-start.4) | collective-permute-done | bytes 131104 | tf_op jit(solution)/shard_map/ppermute | solution.py:139
  159.3 0.7 copy.38
  (54 shorter events, 3.0 us)
Async XLA Ops:
  0.6 3.1 %copy-start.2 = (bf16[512,1024]{1,0:T(8,128)(2,1)S(1)}, bf16[512,1024]{1,0:T(8,128)(2,1)}, u32[]{:S(2)}) copy-start(bf16[512,1024]{1,0:T(8,128)(2,1)} %param.3) | copy-start | bytes 3145732
  6.8 11.5 %copy-start.3 = (bf16[512,1024]{1,0:T(8,128)(2,1)S(1)}, bf16[512,1024]{1,0:T(8,128)(2,1)}, u32[]{:S(2)}) copy-start(bf16[512,1024]{1,0:T(8,128)(2,1)} %param.5) | copy-start | bytes 3145732
  6.8 41.8 %all-to-all-start = ((bf16[128,8,1024]{2,1,0:T(8,128)(2,1)}), bf16[128,8,1024]{2,1,0:T(8,128)(2,1)S(1)}, u32[]{:S(2)}, u32[]{:S(2)}) async-start(bf16[128,8,1024]{2,1,0:T(8,128)(2,1)} %select_bitcast_fusion), calls=%async_computation | async-start | bytes 4194304 | tf_op jit(solution)/shard_map/all_to_all | solution.py:59
  18.3 3.6 %collective-permute-start = (bf16[512,1024]{1,0:T(8,128)(2,1)S(1)}, bf16[512,1024]{1,0:T(8,128)(2,1)}, u32[]{:S(2)}, u32[]{:S(2)}) collective-permute-start(bf16[512,1024]{1,0:T(8,128)(2,1)S(1)} %copy-done.3), channel_id=1, source_target_pairs={{0,16},{16,0},{1,17},{17,1},{2,18},{18,2},{3,19},{19,3},{4,20},{20... | collective-permute-start | bytes 3145736 | tf_op jit(solution)/shard_map/ppermute | solution.py:34
  48.6 2.8 %copy-start = (bf16[128,8,1024]{2,1,0:T(8,128)(2,1)}, bf16[128,8,1024]{2,1,0:T(8,128)(2,1)S(1)}, u32[]{:S(2)}) copy-start(bf16[128,8,1024]{2,1,0:T(8,128)(2,1)S(1)} %all-to-all-done) | copy-start | bytes 6291460
  56.8 3.8 %collective-permute-start.1 = (f32[8,32896]{1,0:T(8,128)}, f32[8,32896]{1,0:T(8,128)S(1)}, u32[]{:S(2)}, u32[]{:S(2)}) collective-permute-start(f32[8,32896]{1,0:T(8,128)} %fusion.15), channel_id=1, source_target_pairs={{0,16},{16,0},{1,17},{17,1},{2,18},{18,2},{3,19},{19,3},{4,20},{20... | collective-permute-start | bytes 3158024 | tf_op jit(solution)/shard_map/ppermute | solution.py:94
  62.4 19.4 %all-to-all-start.1 = ((f32[8,1,32896]{2,1,0:T(1,128)}), f32[8,1,32896]{2,1,0:T(1,128)S(1)}, u32[]{:S(2)}, u32[]{:S(2)}) async-start(f32[8,1,32896]{2,1,0:T(1,128)} %all_to_all.32), calls=%async_computation.1 | async-start | bytes 2105344 | tf_op jit(solution)/shard_map/all_to_all | solution.py:98
  96.7 3.8 %collective-permute-start.2 = (bf16[8,32,1152]{2,1,0:T(8,128)(2,1)S(1)}, bf16[8,32,1152]{2,1,0:T(8,128)(2,1)S(1)}, u32[]{:S(2)}, u32[]{:S(2)}) collective-permute-start(bf16[8,32,1152]{2,1,0:T(8,128)(2,1)S(1)} %all_to_all.45), channel_id=1, source_target_pairs={{0,16},{16,0},{1,17},{17,1},{2,18},{18,2},{3,19},{19,3},{4,20},{20... | collective-permute-start | bytes 1769480 | tf_op jit(solution)/shard_map/ppermute | solution.py:126
  100.7 1.6 copy-start.1
  110.4 20.6 %collective-permute-start.3 = (f32[8,32896]{1,0:T(8,128)}, f32[8,32896]{1,0:T(8,128)S(1)}, u32[]{:S(2)}, u32[]{:S(2)}) collective-permute-start(f32[8,32896]{1,0:T(8,128)} %fusion.10), channel_id=1, source_target_pairs={{0,16},{16,0},{1,17},{17,1},{2,18},{18,2},{3,19},{19,3},{4,20},{20... | collective-permute-start | bytes 3158024 | tf_op jit(solution)/shard_map/ppermute | solution.py:94
  151.6 7.8 %collective-permute-start.4 = (f32[32,1024]{1,0:T(8,128)S(1)}, f32[32,1024]{1,0:T(8,128)S(1)}, u32[]{:S(2)}, u32[]{:S(2)}) collective-permute-start(f32[32,1024]{1,0:T(8,128)S(1)} %add_divide_fusion), channel_id=1, source_target_pairs={{0,0},{8,16},{16,8},{24,24},{1,1},{9,17},{17,9},{25,25},{2,2},{10,... | collective-permute-start | bytes 393224 | tf_op jit(solution)/shard_map/ppermute | solution.py:139
